TPU v7x, 256 devices: a whole 4x4x8 slice. The times are simulated.
256 devices in a mesh: tm: 8 (over z), space: 16 (over y, x), branch: 2 (over core).
Axes of the slice: x: 4, y: 4, z: 8, core: 2. Of those that a mesh axis runs over, the one named last changes fastest.
Arguments:
- state: float32 [2, 8, 2, 256, 1024], P('branch', 'tm', None, 'space'), may hold values from -13 to 15
- panel: float32 [2, 8, 16, 2, 256, 1024], P('branch', 'tm', None, None, 'space'), may hold values from -4 to 4
- region: int32 [256, 1024], P('space'), may hold values from 0 to 5
- feed_table: float32 [6], replicated, may hold values from 0.5 to 2.5
- step_counts: int32 [8], P('tm'), may hold values from 2 to 5, as said below
Outputs:
- deflated: float32 [2, 8, 2, 256, 1024], P('branch', 'tm', None, 'space')
- correction: float32 [2, 8, 2, 256, 1024], P('branch', 'tm', None, 'space')
- coefficients: float32 [2, 16], P('branch')
Inputs may be any that keep to these rules, and one draw needn't show every extreme that they name: `step_counts`: some segment takes 5 steps.
All inputs are finite; a program needn't handle non-finite values.
Results may differ from a plain program's by a relative error of at most 0.0003.
Values sent between devices are 32-bit elements; how exact they have to be, the bound alone decides.
No kernel may reach another device: no remote copies, remote signals or barrier semaphores. Data moves between devices by JAX's collectives and lax.ppermute only.
A program may use at most 64 MiB of HBM per device.

v0:
```python
import functools

import jax
import jax.numpy as jnp
from jax import lax
from jax.sharding import Mesh
from jax.sharding import PartitionSpec as P
from jax.experimental import pallas as pl

STEPS = 5
SPACE = ("space_0", "space_1")
TM_SPACE = ("tm", "space_0", "space_1")


TIME_STEP = 0.03
ACTIVATOR_DIFFUSION = 1.0
INHIBITOR_DIFFUSION = 6.0
REACTION_RATE = 2.5
SMALL_EPSILON = 1e-06
HIGHEST = lax.Precision.HIGHEST
HIGH = lax.Precision.HIGH


def extended_2(cells, sides, width):
    for axis, dim in sides:
        count = lax.axis_size(axis)
        head = lax.slice_in_dim(cells, 0, width, axis=dim)
        tail = lax.slice_in_dim(cells, cells.shape[dim] - width, cells.shape[dim], axis=dim)
        cells = jnp.concatenate(
            [
                lax.ppermute(tail, axis, [(i, (i + 1) % count) for i in range(count)]),
                cells,
                lax.ppermute(head, axis, [((i + 1) % count, i) for i in range(count)]),
            ],
            axis=dim,
        )
    return cells


def swapped(value, axis, apart):
    mask = 2**apart
    pairs = [(source, source ^ mask) for source in range(lax.axis_size(axis))]
    return lax.ppermute(value, axis, pairs)


def passed_along(block, axis, distance):
    devices = range(lax.axis_size(axis))
    route = [((i - distance) % len(devices), i) for i in devices]
    return lax.ppermute(block, axis, route)


def butterfly_rounds(axes):
    rounds = []
    for axis in axes:
        count = lax.axis_size(axis)
        apart = 1
        while apart < count:
            rounds.append((axis, [(i, i ^ apart) for i in range(count)]))
            apart *= 2
    return rounds


def one_axis_at_a_time(x, axes):
    for axis, pairs in butterfly_rounds(axes):
        x = x + lax.ppermute(x, axis, pairs)
    return x


def laplacian_rows(extended):
    interior = extended[..., 1:-1, :]
    return (
        extended[..., 2:, :]
        + extended[..., :-2, :]
        + jnp.roll(interior, 1, -1)
        + jnp.roll(interior, -1, -1)
        - 4.0 * interior
    )


def advance(fields, feed_rate, active):
    activator_wide, inhibitor_wide, tangent_act_wide, tangent_inh_wide = fields
    activator = activator_wide[1:-1]
    inhibitor = inhibitor_wide[1:-1]
    tangent_act = tangent_act_wide[:, 1:-1]
    tangent_inh = tangent_inh_wide[:, 1:-1]
    squared = activator * activator
    product = activator * inhibitor
    new_activator = activator + TIME_STEP * (
        ACTIVATOR_DIFFUSION * laplacian_rows(activator_wide)
        + feed_rate
        - (REACTION_RATE + 1.0) * activator
        + squared * inhibitor
    )
    new_inhibitor = inhibitor + TIME_STEP * (
        INHIBITOR_DIFFUSION * laplacian_rows(inhibitor_wide)
        + REACTION_RATE * activator
        - squared * inhibitor
    )
    new_tangent_act = tangent_act + TIME_STEP * (
        ACTIVATOR_DIFFUSION * laplacian_rows(tangent_act_wide)
        + (2.0 * product - REACTION_RATE - 1.0) * tangent_act
        + squared * tangent_inh
    )
    new_tangent_inh = tangent_inh + TIME_STEP * (
        INHIBITOR_DIFFUSION * laplacian_rows(tangent_inh_wide)
        + (REACTION_RATE - 2.0 * product) * tangent_act
        - squared * tangent_inh
    )
    return (
        jnp.where(active, new_activator, activator),
        jnp.where(active, new_inhibitor, inhibitor),
        jnp.where(active, new_tangent_act, tangent_act),
        jnp.where(active, new_tangent_inh, tangent_inh),
    )


def cholesky_kernel(gram, rhs, out_ref):
    size = gram.shape[0]
    tile = gram
    rows = lax.broadcasted_iota(jnp.int32, tile.shape, 0)
    cols = lax.broadcasted_iota(jnp.int32, tile.shape, 1)
    diagonal = rows == cols
    index = rows[:, :1]
    columns = []
    pivots = []
    for outer in range(size):
        value = jnp.sum(jnp.where(cols == outer, tile, 0.0), axis=1, keepdims=True)
        pivot = jnp.sqrt(jnp.sum(jnp.where(index == outer, value, 0.0), axis=0, keepdims=True))
        column = jnp.where(index >= outer, value / pivot, 0.0)
        row = jnp.sum(jnp.where(diagonal, column, 0.0), axis=0, keepdims=True)
        tile = tile - column * row
        columns.append(column)
        pivots.append(pivot)
    accum = -jnp.sum(jnp.where(diagonal, rhs, 0.0), axis=1, keepdims=True)
    middle = jnp.zeros_like(accum)
    for outer in range(size):
        value = jnp.sum(jnp.where(index == outer, accum, 0.0), axis=0, keepdims=True) / pivots[outer]
        middle = jnp.where(index == outer, value, middle)
        accum = accum - columns[outer] * value
    result = jnp.zeros_like(middle)
    for outer in range(size - 1, -1, -1):
        below = jnp.sum(jnp.where(index > outer, columns[outer] * result, 0.0), axis=0, keepdims=True)
        value = jnp.sum(jnp.where(index == outer, middle, 0.0), axis=0, keepdims=True)
        result = jnp.where(index == outer, (value - below) / pivots[outer], result)
    out_ref[...] = jnp.sum(jnp.where(diagonal, result, 0.0), axis=0, keepdims=True)[:, :size]


def assembly_kernel(jacobian_ref, vectors_ref, out_ref, deflator_ref, *, total):
    vectors = vectors_ref[...]
    lanes = lax.broadcasted_iota(jnp.int32, (1, vectors.shape[1]), 1)
    gap_sum = jnp.sum(jnp.where(lanes == 0, vectors[2:3], 0.0), axis=1, keepdims=True)
    mismatch_sum = jnp.sum(jnp.where(lanes == 1, vectors[2:3], 0.0), axis=1, keepdims=True)
    distance = gap_sum / total + SMALL_EPSILON
    deflator = 1.0 / distance + 1.0
    slopes_row = -2.0 * (vectors[0:1] / total) / (distance * distance)
    cross_row = vectors[1:2]
    tile = jacobian_ref[...]
    rows = lax.broadcasted_iota(jnp.int32, tile.shape, 0)
    cols = lax.broadcasted_iota(jnp.int32, tile.shape, 1)
    diagonal = rows == cols
    slopes_col = jnp.sum(jnp.where(diagonal, slopes_row, 0.0), axis=1, keepdims=True)
    cross_col = jnp.sum(jnp.where(diagonal, cross_row, 0.0), axis=1, keepdims=True)
    gram = (
        deflator * deflator * tile
        + deflator * slopes_col * cross_row
        + deflator * cross_col * slopes_row
        + slopes_col * slopes_row * mismatch_sum
    ) / total
    rhs = (deflator * deflator * cross_row + deflator * slopes_row * mismatch_sum) / total
    cholesky_kernel(gram, rhs, out_ref)
    deflator_ref[...] = deflator


def solve_small(jacobian_sum, along_sum, cross_sum, gap_sum, mismatch_sum, total):
    size = jacobian_sum.shape[0]
    lanes = 128
    padded = jnp.pad(jacobian_sum, ((0, 0), (0, lanes - size)))
    scalars = jnp.stack([gap_sum, mismatch_sum])
    vectors = jnp.stack(
        [
            jnp.pad(along_sum, (0, lanes - size)),
            jnp.pad(cross_sum, (0, lanes - size)),
            jnp.pad(scalars, (0, lanes - 2)),
        ],
        0,
    )
    return pl.pallas_call(
        functools.partial(assembly_kernel, total=total),
        out_shape=(
            jax.ShapeDtypeStruct((1, size), jnp.float32),
            jax.ShapeDtypeStruct((1, 1), jnp.float32),
        ),
    )(padded, vectors)


def on_device(state, panel, region, feed_table, step_counts):
    start = state[0, 0]
    row_count = start.shape[1]
    column_count = start.shape[2]
    directions = panel.shape[2]
    tangent = panel[0, 0].reshape(2 * directions, row_count, column_count)
    stacked = jnp.concatenate([start, tangent], 0)
    following = passed_along(stacked, "tm", -1)
    partner_state = swapped(start, "branch", 0)
    classes = jnp.arange(feed_table.shape[0], dtype=jnp.int32)
    feed_rate = jnp.sum(
        jnp.where(region[None] == classes[:, None, None], feed_table[:, None, None], 0.0), 0
    )
    step_limit = step_counts[0]
    panel_rows = panel[0, 0].reshape(directions, -1)
    gap = (start - partner_state).reshape(-1)
    total = 2.0 * lax.axis_size("tm") * row_count * lax.axis_size(SPACE) * column_count
    gap_part = jnp.sum(gap * gap)
    along_part = jnp.sum(panel_rows * gap[None, :], 1)
    first_sum = jnp.concatenate([gap_part[None], along_part])
    widened = extended_2(jnp.concatenate([stacked, feed_rate[None]], 0), ((SPACE, 1),), STEPS)
    fields = (widened[0], widened[1], widened[2:-1:2], widened[3:-1:2])
    feed_wide = widened[-1]
    total_rows = feed_wide.shape[0]
    for step_index in range(STEPS):
        fields = advance(
            fields,
            feed_wide[step_index + 1 : total_rows - step_index - 1],
            step_index < step_limit,
        )
    end_state = jnp.stack(fields[:2], 0)
    end_tangent = jnp.stack(fields[2:], 1).reshape(directions, -1)
    arrived = passed_along(end_state, "tm", 1)
    next_mismatch = (end_state - following[:2]).reshape(-1)
    next_jacobian = end_tangent - following[2:].reshape(directions, -1)
    jacobian_gram = jnp.dot(next_jacobian, next_jacobian.T, precision=HIGH)
    jacobian_mismatch = jnp.sum(next_jacobian * next_mismatch[None, :], 1)
    mismatch_square = jnp.sum(next_mismatch * next_mismatch)
    moments = one_axis_at_a_time(
        jnp.concatenate(
            [first_sum, mismatch_square[None], jacobian_mismatch, jacobian_gram.reshape(-1)]
        ),
        TM_SPACE,
    )
    gap_sum = moments[0]
    along_sum = moments[1 : 1 + directions]
    mismatch_sum = moments[1 + directions]
    cross_sum = moments[2 + directions : 2 + 2 * directions]
    jacobian_sum = moments[2 + 2 * directions :].reshape(directions, directions)
    coefficients, deflator = solve_small(
        jacobian_sum, along_sum, cross_sum, gap_sum, mismatch_sum, total
    )
    mismatch = (arrived - start).reshape(-1)
    deflated = deflator.reshape(()) * mismatch
    correction = jnp.sum(coefficients.reshape(directions, 1, 1, 1) * panel[0, 0], 0)
    return (
        deflated.reshape(1, 1, 2, row_count, column_count),
        correction.reshape(1, 1, 2, row_count, column_count),
        coefficients.reshape(1, directions),
    )


def solution(mesh):
    finer = Mesh(
        mesh.devices.reshape(mesh.shape["tm"], 4, 4, mesh.shape["branch"]),
        ("tm", "space_0", "space_1", "branch"),
    )
    in_specs = (
        P("branch", "tm", None, SPACE, None),
        P("branch", "tm", None, None, SPACE, None),
        P(SPACE, None),
        P(),
        P("tm"),
    )
    out_specs = (
        P("branch", "tm", None, SPACE, None),
        P("branch", "tm", None, SPACE, None),
        P("branch", None),
    )
    return jax.shard_map(
        on_device, mesh=finer, in_specs=in_specs, out_specs=out_specs, check_vma=False
    )
```

profile of v0, /device:TPU:2, one launch (start us, length us, event | category | flops | bytes accessed | tf_op | source)
XLA Modules:
  0.0 111.6 jit_solution(10774061459842200598)
XLA Ops:
  0.6 1.0 select_reduce_fusion
  1.6 1.7 %pad_maximum_fusion.1 = f32[35,16,1024]{2,1,0:T(8,128)S(1)} fusion(f32[1,16,1024]{2,1,0:T(8,128)S(1)} %bitcast.150, f32[32,16,1024]{2,1,0:T(8,128)} %bitcast.142, f32[2,16,1024]{2,1,0:T(8,128)} %bitcast.146), kind=kLoop, calls=%fused_computation.9 | loop fusion | flops 1146880 | bytes 4587520 | tf_op jit(solution)/shard_map/concatenate | solution.py:216
  3.4 0.3 fusion.151
  3.7 0.4 copy.36
  4.2 2.3 %collective-permute-start.2 = (f32[35,5,1024]{2,0,1:T(8,128)S(1)}, f32[35,5,1024]{2,0,1:T(8,128)S(1)}, u32[]{:S(2)}, u32[]{:S(2)}) collective-permute-start(f32[35,5,1024]{2,0,1:T(8,128)S(1)} %copy.36), channel_id=1, source_target_pairs={{2,0},{4,2},{6,4},{8,6},{10,8},{12,10},{14,12},{16,14},{18,16},{20... | collective-permute-start | bytes 2150408 | tf_op jit(solution)/shard_map/ppermute | solution.py:33
  6.5 0.4 copy.35
  7.1 0.1 pad_maximum_fusion.2
  7.3 5.8 %collective-permute-start.3 = (f32[34,16,1024]{2,1,0:T(8,128)S(1)}, f32[34,16,1024]{2,1,0:T(8,128)S(1)}, u32[]{:S(2)}, u32[]{:S(2)}) collective-permute-start(f32[34,16,1024]{2,1,0:T(8,128)S(1)} %pad_maximum_fusion.2), channel_id=1, source_target_pairs={{32,0},{64,32},{96,64},{128,96},{160,128},{192,160},{224,192},{0,2... | collective-permute-start | bytes 6684680 | tf_op jit(solution)/shard_map/ppermute | solution.py:49
  13.7 0.7 multiply_reduce_fusion.2
  14.4 0.3 multiply_reduce_fusion
  14.7 9.5 %collective-permute-done.2 = f32[35,5,1024]{2,0,1:T(8,128)S(1)} collective-permute-done((f32[35,5,1024]{2,0,1:T(8,128)S(1)}, f32[35,5,1024]{2,0,1:T(8,128)S(1)}, u32[]{:S(2)}, u32[]{:S(2)}) %collective-permute-start.2) | collective-permute-done | bytes 716832 | tf_op jit(solution)/shard_map/ppermute | solution.py:33
  24.2 0.4 copy.38
  24.7 3.8 %collective-permute-done.1 = f32[35,5,1024]{2,0,1:T(8,128)S(1)} collective-permute-done((f32[35,5,1024]{2,0,1:T(8,128)S(1)}, f32[35,5,1024]{2,0,1:T(8,128)S(1)}, u32[]{:S(2)}, u32[]{:S(2)}) %collective-permute-start.1) | collective-permute-done | bytes 716832 | tf_op jit(solution)/shard_map/ppermute | solution.py:31
  28.4 0.4 copy.37
  28.9 0.8 pad_maximum_fusion
  29.9 0.2 add_select_fusion.17
  31.3 0.6 fusion.150
  32.5 0.2 fusion.153
  32.7 1.9 %fusion.152 = (f32[16,24,1023]{2,1,0:T(8,128)S(1)}, f32[16,24,1023]{2,1,0:T(8,128)S(1)}, f32[16,24,1023]{2,1,0:T(8,128)S(1)}, f32[16,24,1023]{2,1,0:T(8,128)S(1)}) fusion(f32[16,26,1024]{2,1,0:T(8,128)S(1)} %get-tuple-element.18, f32[16,26,1024]{2,1,0:T(8,128)S(1)} %get-tuple-element.19), kind=kLoop, calls=%fused_computation.247 | loop fusion | bytes 12570624 | tf_op jit(solution)/shard_map/jit(_roll_static)/slice | solution.py:75
  34.6 1.2 %add_select_fusion.6 = f32[16,24,1024]{2,1,0:T(8,128)S(1)} fusion(f32[16,26,1024]{2,1,0:T(8,128)S(1)} %get-tuple-element.19, f32[16,24,1023]{2,1,0:T(8,128)S(1)} %get-tuple-element.129, f32[16,24,1]{2,1,0:T(8,128)S(1)} %get-tuple-element.131, f32[16,24,1]{2,1,0:T(8,128)S(1)} %get-tuple-element.132, f32[16,24,1023]{2,1,0:T(8,128)S(1)} %get-tuple-element.130, ...), kind=kLoop, calls=%fused_computation.7 | loop fusion | flops 5898240 | bytes 11206657 | tf_op jit(solution)/shard_map/jit(_where)/select_n | solution.py:113
  36.0 0.7 fusion.170
  36.7 1.2 %add_select_fusion.7 = f32[16,24,1024]{2,1,0:T(8,128)S(1)} fusion(f32[16,26,1024]{2,1,0:T(8,128)S(1)} %get-tuple-element.18, f32[16,24,1023]{2,1,0:T(8,128)S(1)} %get-tuple-element.25, f32[16,24,1]{2,1,0:T(8,128)S(1)} %get-tuple-element.27, f32[16,24,1]{2,1,0:T(8,128)S(1)} %get-tuple-element.26, f32[16,24,1023]{2,1,0:T(8,128)S(1)} %get-tuple-element.24, ...), kind=kLoop, calls=%fused_computation.8 | loop fusion | flops 5505024 | bytes 11206657 | tf_op jit(solution)/shard_map/jit(_where)/select_n | solution.py:112
  38.0 1.3 %add_select_fusion.4 = f32[16,22,1024]{2,1,0:T(8,128)S(1)} fusion(f32[16,24,1024]{2,1,0:T(8,128)S(1)} %add_select_fusion.6, f32[16,22,1023]{2,1,0:T(8,128)S(1)} %get-tuple-element.61, f32[16,22,1]{2,1,0:T(8,128)S(1)} %get-tuple-element.63, f32[16,22,1]{2,1,0:T(8,128)S(1)} %get-tuple-element.62, f32[16,22,1023]{2,1,0:T(8,128)S(1)} %get-tuple-element.60, ...), kind=kLoop, calls=%fused_computation.5 | loop fusion | flops 5406720 | bytes 10272769 | tf_op jit(solution)/shard_map/jit(_where)/select_n | solution.py:113
  39.4 0.7 fusion.168
  40.1 0.7 fusion.166
  40.8 1.5 %add_select_fusion.5 = f32[16,22,1024]{2,1,0:T(8,128)S(1)} fusion(f32[16,24,1024]{2,1,0:T(8,128)S(1)} %add_select_fusion.7, f32[16,22,1023]{2,1,0:T(8,128)S(1)} %get-tuple-element.53, f32[16,22,1]{2,1,0:T(8,128)S(1)} %get-tuple-element.55, f32[16,22,1]{2,1,0:T(8,128)S(1)} %get-tuple-element.54, f32[16,22,1023]{2,1,0:T(8,128)S(1)} %get-tuple-element.52, ...), kind=kLoop, calls=%fused_computation.6 | loop fusion | flops 5046272 | bytes 10272769 | tf_op jit(solution)/shard_map/jit(_where)/select_n | solution.py:112
  42.5 1.3 %add_select_fusion.2 = f32[16,20,1024]{2,1,0:T(8,128)S(1)} fusion(f32[16,22,1024]{2,1,0:T(8,128)S(1)} %add_select_fusion.4, f32[16,20,1023]{2,1,0:T(8,128)S(1)} %get-tuple-element.57, f32[16,20,1]{2,1,0:T(8,128)S(1)} %get-tuple-element.59, f32[16,20,1]{2,1,0:T(8,128)S(1)} %get-tuple-element.58, f32[16,20,1023]{2,1,0:T(8,128)S(1)} %get-tuple-element.56, ...), kind=kLoop, calls=%fused_computation.3 | loop fusion | flops 4915200 | bytes 9338881 | tf_op jit(solution)/shard_map/jit(_where)/select_n | solution.py:113
  43.9 0.7 fusion.164
  44.6 0.7 fusion.162
  45.3 1.3 %add_select_fusion.3 = f32[16,20,1024]{2,1,0:T(8,128)S(1)} fusion(f32[16,22,1024]{2,1,0:T(8,128)S(1)} %add_select_fusion.5, f32[16,20,1023]{2,1,0:T(8,128)S(1)} %get-tuple-element.45, f32[16,20,1]{2,1,0:T(8,128)S(1)} %get-tuple-element.47, f32[16,20,1]{2,1,0:T(8,128)S(1)} %get-tuple-element.46, f32[16,20,1023]{2,1,0:T(8,128)S(1)} %get-tuple-element.44, ...), kind=kLoop, calls=%fused_computation.4 | loop fusion | flops 4587520 | bytes 9338881 | tf_op jit(solution)/shard_map/jit(_where)/select_n | solution.py:112
  46.7 0.7 fusion.158
  47.4 1.3 %add_select_fusion = f32[16,18,1024]{2,1,0:T(8,128)S(1)} fusion(f32[16,20,1024]{2,1,0:T(8,128)S(1)} %add_select_fusion.2, f32[16,18,1023]{2,1,0:T(8,128)S(1)} %get-tuple-element.49, f32[16,18,1]{2,1,0:T(8,128)S(1)} %get-tuple-element.51, f32[16,18,1]{2,1,0:T(8,128)S(1)} %get-tuple-element.50, f32[16,18,1023]{2,1,0:T(8,128)S(1)} %get-tuple-element.48, ...), kind=kLoop, calls=%fused_computation.1 | loop fusion | flops 4423680 | bytes 8404993 | tf_op jit(solution)/shard_map/jit(_where)/select_n | solution.py:113
  48.9 1.3 %add_select_fusion.1 = f32[16,18,1024]{2,1,0:T(8,128)S(1)} fusion(f32[16,20,1024]{2,1,0:T(8,128)S(1)} %add_select_fusion.3, f32[16,18,1023]{2,1,0:T(8,128)S(1)} %get-tuple-element.37, f32[16,18,1]{2,1,0:T(8,128)S(1)} %get-tuple-element.39, f32[16,18,1]{2,1,0:T(8,128)S(1)} %get-tuple-element.38, f32[16,18,1023]{2,1,0:T(8,128)S(1)} %get-tuple-element.36, ...), kind=kLoop, calls=%fused_computation.2 | loop fusion | flops 4128768 | bytes 8404993 | tf_op jit(solution)/shard_map/jit(_where)/select_n | solution.py:112
  50.5 0.5 fusion.160
  51.0 0.5 fusion.156
  51.4 0.8 fusion.59
  52.3 0.8 fusion.60
  53.1 0.2 pad_maximum_fusion.3
  53.7 7.7 %collective-permute-done.3 = f32[34,16,1024]{2,1,0:T(8,128)S(1)} collective-permute-done((f32[34,16,1024]{2,1,0:T(8,128)S(1)}, f32[34,16,1024]{2,1,0:T(8,128)S(1)}, u32[]{:S(2)}, u32[]{:S(2)}) %collective-permute-start.3) | collective-permute-done | bytes 2228256 | tf_op jit(solution)/shard_map/ppermute | solution.py:49
  61.4 0.6 multiply_reduce_fusion.1
  62.0 0.4 fusion.1
  62.5 3.1 %fusion.56 = f32[16,16]{1,0:T(8,128)S(1)} fusion(f32[16,2,16,1024]{3,2,1,0:T(8,128)S(1)} %bitcast.145), kind=kOutput, calls=%fused_computation.86 | convolution fusion | flops 50331648 | bytes 2098176 | tf_op jit(solution)/shard_map/dot_general | solution.py:231
  65.9 1.4 %concatenate.196 = f32[290]{0:T(512)S(1)} concatenate(f32[1]{0:T(128)} %bitcast.1, f32[16]{0:T(128)S(1)} %multiply_reduce_fusion, f32[1]{0:T(128)} %bitcast.19, f32[16]{0:T(128)S(1)} %reduce_sum.67, f32[256]{0:T(256)S(1)} %reshape.91), dimensions={0} | concatenate | bytes 2320 | tf_op jit(solution)/shard_map/concatenate | solution.py:235
  67.4 3.6 %collective-permute-done.4 = f32[290]{0:T(512)S(1)} collective-permute-done((f32[290]{0:T(512)S(1)}, f32[290]{0:T(512)S(1)}, u32[]{:S(2)}, u32[]{:S(2)}) %collective-permute-start.4) | collective-permute-done | bytes 1192 | tf_op jit(solution)/shard_map/ppermute | solution.py:65
  70.9 1.2 %collective-permute-start.5 = (f32[290]{0:T(512)S(1)}, f32[290]{0:T(512)S(1)}, u32[]{:S(2)}, u32[]{:S(2)}) collective-permute-start(f32[290]{0:T(512)S(1)} %add.499), channel_id=1, source_target_pairs={{0,64},{32,96},{64,0},{96,32},{128,192},{160,224},{192,128},{224,1... | collective-permute-start | bytes 3488 | tf_op jit(solution)/shard_map/ppermute | solution.py:65
  72.1 3.3 %collective-permute-done.5 = f32[290]{0:T(512)S(1)} collective-permute-done((f32[290]{0:T(512)S(1)}, f32[290]{0:T(512)S(1)}, u32[]{:S(2)}, u32[]{:S(2)}) %collective-permute-start.5) | collective-permute-done | bytes 1192 | tf_op jit(solution)/shard_map/ppermute | solution.py:65
  75.4 3.8 %collective-permute-start.6 = (f32[290]{0:T(512)S(1)}, f32[290]{0:T(512)S(1)}, u32[]{:S(2)}, u32[]{:S(2)}) collective-permute-start(f32[290]{0:T(512)S(1)} %add.500), channel_id=1, source_target_pairs={{0,128},{32,160},{64,192},{96,224},{128,0},{160,32},{192,64},{224,... | collective-permute-start | bytes 3488 | tf_op jit(solution)/shard_map/ppermute | solution.py:65
  79.2 3.7 %collective-permute-done.6 = f32[290]{0:T(512)S(1)} collective-permute-done((f32[290]{0:T(512)S(1)}, f32[290]{0:T(512)S(1)}, u32[]{:S(2)}, u32[]{:S(2)}) %collective-permute-start.6) | collective-permute-done | bytes 1192 | tf_op jit(solution)/shard_map/ppermute | solution.py:65
  82.9 1.6 %collective-permute-start.7 = (f32[290]{0:T(512)S(1)}, f32[290]{0:T(512)S(1)}, u32[]{:S(2)}, u32[]{:S(2)}) collective-permute-start(f32[290]{0:T(512)S(1)} %add.501), channel_id=1, source_target_pairs={{0,8},{8,0},{16,24},{24,16},{1,9},{9,1},{17,25},{25,17},{2,10},{10... | collective-permute-start | bytes 3488 | tf_op jit(solution)/shard_map/ppermute | solution.py:65
  84.5 2.0 %collective-permute-done.7 = f32[290]{0:T(512)S(1)} collective-permute-done((f32[290]{0:T(512)S(1)}, f32[290]{0:T(512)S(1)}, u32[]{:S(2)}, u32[]{:S(2)}) %collective-permute-start.7) | collective-permute-done | bytes 1192 | tf_op jit(solution)/shard_map/ppermute | solution.py:65
  86.5 3.2 %collective-permute-start.8 = (f32[290]{0:T(512)S(1)}, f32[290]{0:T(512)S(1)}, u32[]{:S(2)}, u32[]{:S(2)}) collective-permute-start(f32[290]{0:T(512)S(1)} %add.502), channel_id=1, source_target_pairs={{0,16},{8,24},{16,0},{24,8},{1,17},{9,25},{17,1},{25,9},{2,18},{10... | collective-permute-start | bytes 3488 | tf_op jit(solution)/shard_map/ppermute | solution.py:65
  89.7 1.9 %collective-permute-done.8 = f32[290]{0:T(512)S(1)} collective-permute-done((f32[290]{0:T(512)S(1)}, f32[290]{0:T(512)S(1)}, u32[]{:S(2)}, u32[]{:S(2)}) %collective-permute-start.8) | collective-permute-done | bytes 1192 | tf_op jit(solution)/shard_map/ppermute | solution.py:65
  91.6 3.8 %collective-permute-start.9 = (f32[290]{0:T(512)S(1)}, f32[290]{0:T(512)S(1)}, u32[]{:S(2)}, u32[]{:S(2)}) collective-permute-start(f32[290]{0:T(512)S(1)} %add.503), channel_id=1, source_target_pairs={{0,2},{2,0},{4,6},{6,4},{1,3},{3,1},{5,7},{7,5},{8,10},{10,8},{12,... | collective-permute-start | bytes 3488 | tf_op jit(solution)/shard_map/ppermute | solution.py:65
  95.4 1.6 %collective-permute-done.9 = f32[290]{0:T(512)S(1)} collective-permute-done((f32[290]{0:T(512)S(1)}, f32[290]{0:T(512)S(1)}, u32[]{:S(2)}, u32[]{:S(2)}) %collective-permute-start.9) | collective-permute-done | bytes 1192 | tf_op jit(solution)/shard_map/ppermute | solution.py:65
  97.0 2.6 %collective-permute-start.10 = (f32[290]{0:T(512)S(1)}, f32[290]{0:T(512)S(1)}, u32[]{:S(2)}, u32[]{:S(2)}) collective-permute-start(f32[290]{0:T(512)S(1)} %add.504), channel_id=1, source_target_pairs={{0,4},{2,6},{4,0},{6,2},{1,5},{3,7},{5,1},{7,3},{8,12},{10,14},{12... | collective-permute-start | bytes 3488 | tf_op jit(solution)/shard_map/ppermute | solution.py:65
  99.6 0.3 collective-permute-start.11
  99.8 2.2 %collective-permute-done.10 = f32[290]{0:T(512)S(1)} collective-permute-done((f32[290]{0:T(512)S(1)}, f32[290]{0:T(512)S(1)}, u32[]{:S(2)}, u32[]{:S(2)}) %collective-permute-start.10) | collective-permute-done | bytes 1192 | tf_op jit(solution)/shard_map/ppermute | solution.py:65
  102.2 0.6 fusion.193
  102.9 0.6 pad.15.jacobian_ref
  103.5 1.4 %fusion.149 = f32[1,128]{1,0:T(1,128)S(1)} fusion(f32[1]{0:T(128)} %get-tuple-element.124, f32[1]{0:T(128)} %get-tuple-element.123), kind=kLoop, calls=%fused_computation.243 | loop fusion | flops 512 | bytes 520 | tf_op jit(solution)/shard_map/stack | solution.py:179
  104.9 0.6 pad_maximum_fusion.5.vectors_ref
  105.5 3.3 %shard_map.76 = (f32[1,16]{1,0:T(1,128)}, f32[1,1]{1,0:T(1,128)}) custom-call(f32[16,128]{1,0:T(8,128)} %pad.15.jacobian_ref, f32[3,128]{1,0:T(4,128)} %pad_maximum_fusion.5.vectors_ref), custom_call_target="tpu_custom_call" | custom-call | tf_op jit(solution)/shard_map/pallas_call | solution.py:187
  108.7 1.6 %fusion = f32[2,16,1024]{2,1,0:T(8,128)} fusion(f32[1,1,16,2,16,1024]{5,4,3,2,1,0:T(8,128)S(1)} %copy-done, f32[16]{0:T(128)} %bitcast.153), kind=kLoop, calls=%fused_computation.14 | loop fusion | flops 1015808 | bytes 2228288 | tf_op jit(solution)/shard_map/reduce_sum | solution.py:250
  110.3 1.3 %multiply_bitcast_fusion = f32[1,1,2,16,1024]{4,3,2,1,0:T(8,128)} fusion(f32[2,16,1024]{2,1,0:T(8,128)S(1)} %collective-permute-done.11, f32[]{:T(128)} %bitcast.33, f32[1,1,2,16,1024]{4,3,2,1,0:T(8,128)S(1)} %copy-done.1), kind=kLoop, calls=%fused_computation.117 | loop fusion | flops 65536 | bytes 393220 | tf_op jit(solution)/shard_map/mul | solution.py:249
  (60 shorter events, 4.3 us)
Async XLA Ops:
  3.7 3.3 %copy-start.1 = (f32[1,1,2,16,1024]{4,3,2,1,0:T(8,128)S(1)}, f32[1,1,2,16,1024]{4,3,2,1,0:T(8,128)}, u32[]{:S(2)}) copy-start(f32[1,1,2,16,1024]{4,3,2,1,0:T(8,128)} %param.5) | copy-start | bytes 393220
  3.7 3.4 %copy-start = (f32[1,1,16,2,16,1024]{5,4,3,2,1,0:T(8,128)S(1)}, f32[1,1,16,2,16,1024]{5,4,3,2,1,0:T(8,128)}, u32[]{:S(2)}) copy-start(f32[1,1,16,2,16,1024]{5,4,3,2,1,0:T(8,128)} %param.6) | copy-start | bytes 6291460
  4.2 20.1 %collective-permute-start.2 = (f32[35,5,1024]{2,0,1:T(8,128)S(1)}, f32[35,5,1024]{2,0,1:T(8,128)S(1)}, u32[]{:S(2)}, u32[]{:S(2)}) collective-permute-start(f32[35,5,1024]{2,0,1:T(8,128)S(1)} %copy.36), channel_id=1, source_target_pairs={{2,0},{4,2},{6,4},{8,6},{10,8},{12,10},{14,12},{16,14},{18,16},{20... | collective-permute-start | bytes 2150408 | tf_op jit(solution)/shard_map/ppermute | solution.py:33
  6.9 21.5 %collective-permute-start.1 = (f32[35,5,1024]{2,0,1:T(8,128)S(1)}, f32[35,5,1024]{2,0,1:T(8,128)S(1)}, u32[]{:S(2)}, u32[]{:S(2)}) collective-permute-start(f32[35,5,1024]{2,0,1:T(8,128)S(1)} %copy.35), channel_id=1, source_target_pairs={{0,2},{2,4},{4,6},{6,8},{8,10},{10,12},{12,14},{14,16},{16,18},{18... | collective-permute-start | bytes 2150408 | tf_op jit(solution)/shard_map/ppermute | solution.py:31
  7.0 6.7 %collective-permute-start = (f32[2,16,1024]{2,1,0:T(8,128)S(1)}, f32[2,16,1024]{2,1,0:T(8,128)S(1)}, u32[]{:S(2)}, u32[]{:S(2)}) collective-permute-start(f32[2,16,1024]{2,1,0:T(8,128)S(1)} %bitcast.147), channel_id=1, source_target_pairs={{0,1},{1,0},{2,3},{3,2},{4,5},{5,4},{6,7},{7,6},{8,9},{9,8},{10,11... | collective-permute-start | bytes 393224 | tf_op jit(solution)/shard_map/ppermute | solution.py:43
  7.3 54.1 %collective-permute-start.3 = (f32[34,16,1024]{2,1,0:T(8,128)S(1)}, f32[34,16,1024]{2,1,0:T(8,128)S(1)}, u32[]{:S(2)}, u32[]{:S(2)}) collective-permute-start(f32[34,16,1024]{2,1,0:T(8,128)S(1)} %pad_maximum_fusion.2), channel_id=1, source_target_pairs={{32,0},{64,32},{96,64},{128,96},{160,128},{192,160},{224,192},{0,2... | collective-permute-start | bytes 6684680 | tf_op jit(solution)/shard_map/ppermute | solution.py:49
  67.3 3.6 %collective-permute-start.4 = (f32[290]{0:T(512)S(1)}, f32[290]{0:T(512)S(1)}, u32[]{:S(2)}, u32[]{:S(2)}) collective-permute-start(f32[290]{0:T(512)S(1)} %concatenate.196), channel_id=1, source_target_pairs={{0,32},{32,0},{64,96},{96,64},{128,160},{160,128},{192,224},{224,1... | collective-permute-start | bytes 3488 | tf_op jit(solution)/shard_map/ppermute | solution.py:65
  70.9 4.5 %collective-permute-start.5 = (f32[290]{0:T(512)S(1)}, f32[290]{0:T(512)S(1)}, u32[]{:S(2)}, u32[]{:S(2)}) collective-permute-start(f32[290]{0:T(512)S(1)} %add.499), channel_id=1, source_target_pairs={{0,64},{32,96},{64,0},{96,32},{128,192},{160,224},{192,128},{224,1... | collective-permute-start | bytes 3488 | tf_op jit(solution)/shard_map/ppermute | solution.py:65
  75.4 7.5 %collective-permute-start.6 = (f32[290]{0:T(512)S(1)}, f32[290]{0:T(512)S(1)}, u32[]{:S(2)}, u32[]{:S(2)}) collective-permute-start(f32[290]{0:T(512)S(1)} %add.500), channel_id=1, source_target_pairs={{0,128},{32,160},{64,192},{96,224},{128,0},{160,32},{192,64},{224,... | collective-permute-start | bytes 3488 | tf_op jit(solution)/shard_map/ppermute | solution.py:65
  82.9 3.6 %collective-permute-start.7 = (f32[290]{0:T(512)S(1)}, f32[290]{0:T(512)S(1)}, u32[]{:S(2)}, u32[]{:S(2)}) collective-permute-start(f32[290]{0:T(512)S(1)} %add.501), channel_id=1, source_target_pairs={{0,8},{8,0},{16,24},{24,16},{1,9},{9,1},{17,25},{25,17},{2,10},{10... | collective-permute-start | bytes 3488 | tf_op jit(solution)/shard_map/ppermute | solution.py:65
  86.5 5.1 %collective-permute-start.8 = (f32[290]{0:T(512)S(1)}, f32[290]{0:T(512)S(1)}, u32[]{:S(2)}, u32[]{:S(2)}) collective-permute-start(f32[290]{0:T(512)S(1)} %add.502), channel_id=1, source_target_pairs={{0,16},{8,24},{16,0},{24,8},{1,17},{9,25},{17,1},{25,9},{2,18},{10... | collective-permute-start | bytes 3488 | tf_op jit(solution)/shard_map/ppermute | solution.py:65
  91.6 5.4 %collective-permute-start.9 = (f32[290]{0:T(512)S(1)}, f32[290]{0:T(512)S(1)}, u32[]{:S(2)}, u32[]{:S(2)}) collective-permute-start(f32[290]{0:T(512)S(1)} %add.503), channel_id=1, source_target_pairs={{0,2},{2,0},{4,6},{6,4},{1,3},{3,1},{5,7},{7,5},{8,10},{10,8},{12,... | collective-permute-start | bytes 3488 | tf_op jit(solution)/shard_map/ppermute | solution.py:65
  97.0 5.1 %collective-permute-start.10 = (f32[290]{0:T(512)S(1)}, f32[290]{0:T(512)S(1)}, u32[]{:S(2)}, u32[]{:S(2)}) collective-permute-start(f32[290]{0:T(512)S(1)} %add.504), channel_id=1, source_target_pairs={{0,4},{2,6},{4,0},{6,2},{1,5},{3,7},{5,1},{7,3},{8,12},{10,14},{12... | collective-permute-start | bytes 3488 | tf_op jit(solution)/shard_map/ppermute | solution.py:65
  99.6 10.7 %collective-permute-start.11 = (f32[2,16,1024]{2,1,0:T(8,128)S(1)}, f32[2,16,1024]{2,1,0:T(8,128)S(1)}, u32[]{:S(2)}, u32[]{:S(2)}) collective-permute-start(f32[2,16,1024]{2,1,0:T(8,128)S(1)} %get-tuple-element.76), channel_id=1, source_target_pairs={{224,0},{0,32},{32,64},{64,96},{96,128},{128,160},{160,192},{192,2... | collective-permute-start | bytes 393224 | tf_op jit(solution)/shard_map/ppermute | solution.py:49
where the time goes:
time: 113 us; the launch traced here: 112 us
  waiting for transfers between devices  39.3 us (35%)
  starting transfers between devices  24.7 us (22%)
  other arithmetic  24 us (21%)
  local copies, waits for them, and re-layouts  15.5 us (14%)
  Pallas kernels  3.26 us (3%)
  matrix products  3.13 us (3%)
  between operations  1.72 us (2%)
    ppermute x7, waiting for transfers between devices, one_axis_at_a_time(): x = x + lax.ppermute(x, axis, pairs)  18.3 us
    ppermute x7, starting transfers between devices, one_axis_at_a_time(): x = x + lax.ppermute(x, axis, pairs)  16.2 us
    slice x36, local copies, waits for them, and re-layouts, laplacian_rows(): jnp.roll(interior, -1, -1)  9.66 us
    ppermute x1, waiting for transfers between devices, extended_2(): lax.ppermute(head, axis, [((i + 1) % count, i) for i in range(count)])  9.52 us
    ppermute x2, waiting for transfers between devices, passed_along(): return lax.ppermute(block, axis, route)  7.71 us
    ppermute x2, starting transfers between devices, passed_along(): return lax.ppermute(block, axis, route)  6.06 us
    select_n x4, other arithmetic, advance(): jnp.where(active, new_tangent_act, tangent_act)  5.2 us
    select_n x4, other arithmetic, advance(): jnp.where(active, new_tangent_inh, tangent_inh)  5.2 us
  transfers between devices with their start and end apart: 12, of which 10 were waited for; matrix products, arithmetic and copies ran while one was open for 29% of the time, Pallas kernels for 3%

commit v1 on v0

--- a/solution.py
+++ b/solution.py
@@ -145,15 +145,14 @@
     out_ref[...] = jnp.sum(jnp.where(diagonal, result, 0.0), axis=0, keepdims=True)[:, :size]
 
 
-def assembly_kernel(jacobian_ref, vectors_ref, out_ref, deflator_ref, *, total):
-    vectors = vectors_ref[...]
-    lanes = lax.broadcasted_iota(jnp.int32, (1, vectors.shape[1]), 1)
-    gap_sum = jnp.sum(jnp.where(lanes == 0, vectors[2:3], 0.0), axis=1, keepdims=True)
-    mismatch_sum = jnp.sum(jnp.where(lanes == 1, vectors[2:3], 0.0), axis=1, keepdims=True)
+def assembly_kernel(jacobian_ref, along_ref, cross_ref, scalar_ref, out_ref, deflator_ref, *, total):
+    scalars = scalar_ref[...]
+    gap_sum = scalars[:, 0:1]
+    mismatch_sum = scalars[:, 1:2]
     distance = gap_sum / total + SMALL_EPSILON
     deflator = 1.0 / distance + 1.0
-    slopes_row = -2.0 * (vectors[0:1] / total) / (distance * distance)
-    cross_row = vectors[1:2]
+    slopes_row = -2.0 * (along_ref[...] / total) / (distance * distance)
+    cross_row = cross_ref[...]
     tile = jacobian_ref[...]
     rows = lax.broadcasted_iota(jnp.int32, tile.shape, 0)
     cols = lax.broadcasted_iota(jnp.int32, tile.shape, 1)
@@ -171,26 +170,15 @@
     deflator_ref[...] = deflator
 
 
-def solve_small(jacobian_sum, along_sum, cross_sum, gap_sum, mismatch_sum, total):
+def solve_small(jacobian_sum, along_sum, cross_sum, scalars, total):
     size = jacobian_sum.shape[0]
-    lanes = 128
-    padded = jnp.pad(jacobian_sum, ((0, 0), (0, lanes - size)))
-    scalars = jnp.stack([gap_sum, mismatch_sum])
-    vectors = jnp.stack(
-        [
-            jnp.pad(along_sum, (0, lanes - size)),
-            jnp.pad(cross_sum, (0, lanes - size)),
-            jnp.pad(scalars, (0, lanes - 2)),
-        ],
-        0,
-    )
     return pl.pallas_call(
         functools.partial(assembly_kernel, total=total),
         out_shape=(
             jax.ShapeDtypeStruct((1, size), jnp.float32),
             jax.ShapeDtypeStruct((1, 1), jnp.float32),
         ),
-    )(padded, vectors)
+    )(jacobian_sum, along_sum.reshape(1, size), cross_sum.reshape(1, size), scalars.reshape(1, 2))
 
 
 def on_device(state, panel, region, feed_table, step_counts):
@@ -212,7 +200,6 @@
     total = 2.0 * lax.axis_size("tm") * row_count * lax.axis_size(SPACE) * column_count
     gap_part = jnp.sum(gap * gap)
     along_part = jnp.sum(panel_rows * gap[None, :], 1)
-    first_sum = jnp.concatenate([gap_part[None], along_part])
     widened = extended_2(jnp.concatenate([stacked, feed_rate[None]], 0), ((SPACE, 1),), STEPS)
     fields = (widened[0], widened[1], widened[2:-1:2], widened[3:-1:2])
     feed_wide = widened[-1]
@@ -233,18 +220,21 @@
     mismatch_square = jnp.sum(next_mismatch * next_mismatch)
     moments = one_axis_at_a_time(
         jnp.concatenate(
-            [first_sum, mismatch_square[None], jacobian_mismatch, jacobian_gram.reshape(-1)]
+            [
+                gap_part[None],
+                mismatch_square[None],
+                along_part,
+                jacobian_mismatch,
+                jacobian_gram.reshape(-1),
+            ]
         ),
         TM_SPACE,
     )
-    gap_sum = moments[0]
-    along_sum = moments[1 : 1 + directions]
-    mismatch_sum = moments[1 + directions]
+    scalars = moments[:2]
+    along_sum = moments[2 : 2 + directions]
     cross_sum = moments[2 + directions : 2 + 2 * directions]
     jacobian_sum = moments[2 + 2 * directions :].reshape(directions, directions)
-    coefficients, deflator = solve_small(
-        jacobian_sum, along_sum, cross_sum, gap_sum, mismatch_sum, total
-    )
+    coefficients, deflator = solve_small(jacobian_sum, along_sum, cross_sum, scalars, total)
     mismatch = (arrived - start).reshape(-1)
     deflated = deflator.reshape(()) * mismatch
     correction = jnp.sum(coefficients.reshape(directions, 1, 1, 1) * panel[0, 0], 0)

time: 113 us -> 112 us (level)
  other arithmetic: 24 us -> 22 us
    another operation x2 -> x0, other arithmetic: 1.95 us -> none  [solve_small(): jnp.stack([jnp.pad(along_sum, (0, lanes - size)), jnp.pad(cross_sum, (0,...]
    reshape x0 -> x2, local copies, waits for them, and re-layouts: none -> 1.14 us  [the longest x1 0.59 us: solve_small(): cross_sum.reshape(1, size)]
  transfers between devices with their start and end apart: 12 -> 12, of which waited for: 10 -> 10; matrix products, arithmetic and copies ran while one was open for 29% -> 28% of each run, Pallas kernels for 3% -> 3%
where the time goes in v1:
time: 112 us; the launch traced here: 110 us
  waiting for transfers between devices  39.3 us (35%)
  starting transfers between devices  24.7 us (22%)
  other arithmetic  22 us (20%)
  local copies, waits for them, and re-layouts  15.9 us (14%)
  Pallas kernels  3.36 us (3%)
  matrix products  3.13 us (3%)
  between operations  1.71 us (2%)
    ppermute x7, waiting for transfers between devices, one_axis_at_a_time(): x = x + lax.ppermute(x, axis, pairs)  18.3 us
    ppermute x7, starting transfers between devices, one_axis_at_a_time(): x = x + lax.ppermute(x, axis, pairs)  16.2 us
    slice x36, local copies, waits for them, and re-layouts, laplacian_rows(): jnp.roll(interior, -1, -1)  9.66 us
    ppermute x1, waiting for transfers between devices, extended_2(): lax.ppermute(head, axis, [((i + 1) % count, i) for i in range(count)])  9.57 us
    ppermute x2, waiting for transfers between devices, passed_along(): return lax.ppermute(block, axis, route)  7.71 us
    ppermute x2, starting transfers between devices, passed_along(): return lax.ppermute(block, axis, route)  6.06 us
    select_n x4, other arithmetic, advance(): jnp.where(active, new_tangent_act, tangent_act)  5.2 us
    select_n x4, other arithmetic, advance(): jnp.where(active, new_tangent_inh, tangent_inh)  5.2 us
  transfers between devices with their start and end apart: 12, of which 10 were waited for; matrix products, arithmetic and copies ran while one was open for 28% of the time, Pallas kernels for 3%

profile of v1, /device:TPU:2, one launch (start us, length us, event | category | flops | bytes accessed | tf_op | source)
XLA Modules:
  0.0 110.2 jit_solution(5141517452913070188)
XLA Ops:
  0.6 1.0 select_reduce_fusion
  1.6 1.7 %pad_maximum_fusion.1 = f32[35,16,1024]{2,1,0:T(8,128)S(1)} fusion(f32[1,16,1024]{2,1,0:T(8,128)S(1)} %bitcast.150, f32[32,16,1024]{2,1,0:T(8,128)} %bitcast.142, f32[2,16,1024]{2,1,0:T(8,128)} %bitcast.146), kind=kLoop, calls=%fused_computation.9 | loop fusion | flops 1146880 | bytes 4587520 | tf_op jit(solution)/shard_map/concatenate | solution.py:203
  3.4 0.3 fusion.149
  3.7 0.4 copy.36
  4.2 2.3 %collective-permute-start.2 = (f32[35,5,1024]{2,0,1:T(8,128)S(1)}, f32[35,5,1024]{2,0,1:T(8,128)S(1)}, u32[]{:S(2)}, u32[]{:S(2)}) collective-permute-start(f32[35,5,1024]{2,0,1:T(8,128)S(1)} %copy.36), channel_id=1, source_target_pairs={{2,0},{4,2},{6,4},{8,6},{10,8},{12,10},{14,12},{16,14},{18,16},{20... | collective-permute-start | bytes 2150408 | tf_op jit(solution)/shard_map/ppermute | solution.py:33
  6.5 0.4 copy.35
  7.1 0.1 pad_maximum_fusion.2
  7.3 5.8 %collective-permute-start.3 = (f32[34,16,1024]{2,1,0:T(8,128)S(1)}, f32[34,16,1024]{2,1,0:T(8,128)S(1)}, u32[]{:S(2)}, u32[]{:S(2)}) collective-permute-start(f32[34,16,1024]{2,1,0:T(8,128)S(1)} %pad_maximum_fusion.2), channel_id=1, source_target_pairs={{32,0},{64,32},{96,64},{128,96},{160,128},{192,160},{224,192},{0,2... | collective-permute-start | bytes 6684680 | tf_op jit(solution)/shard_map/ppermute | solution.py:49
  13.7 0.6 multiply_reduce_fusion.2
  14.4 0.3 multiply_reduce_fusion
  14.6 9.6 %collective-permute-done.2 = f32[35,5,1024]{2,0,1:T(8,128)S(1)} collective-permute-done((f32[35,5,1024]{2,0,1:T(8,128)S(1)}, f32[35,5,1024]{2,0,1:T(8,128)S(1)}, u32[]{:S(2)}, u32[]{:S(2)}) %collective-permute-start.2) | collective-permute-done | bytes 716832 | tf_op jit(solution)/shard_map/ppermute | solution.py:33
  24.2 0.4 copy.38
  24.7 3.8 %collective-permute-done.1 = f32[35,5,1024]{2,0,1:T(8,128)S(1)} collective-permute-done((f32[35,5,1024]{2,0,1:T(8,128)S(1)}, f32[35,5,1024]{2,0,1:T(8,128)S(1)}, u32[]{:S(2)}, u32[]{:S(2)}) %collective-permute-start.1) | collective-permute-done | bytes 716832 | tf_op jit(solution)/shard_map/ppermute | solution.py:31
  28.4 0.4 copy.37
  28.9 0.8 pad_maximum_fusion
  29.9 0.2 add_select_fusion.17
  31.3 0.6 fusion.148
  32.5 0.2 fusion.151
  32.7 1.9 %fusion.150 = (f32[16,24,1023]{2,1,0:T(8,128)S(1)}, f32[16,24,1023]{2,1,0:T(8,128)S(1)}, f32[16,24,1023]{2,1,0:T(8,128)S(1)}, f32[16,24,1023]{2,1,0:T(8,128)S(1)}) fusion(f32[16,26,1024]{2,1,0:T(8,128)S(1)} %get-tuple-element.18, f32[16,26,1024]{2,1,0:T(8,128)S(1)} %get-tuple-element.19), kind=kLoop, calls=%fused_computation.243 | loop fusion | bytes 12570624 | tf_op jit(solution)/shard_map/jit(_roll_static)/slice | solution.py:75
  34.6 1.2 %add_select_fusion.6 = f32[16,24,1024]{2,1,0:T(8,128)S(1)} fusion(f32[16,26,1024]{2,1,0:T(8,128)S(1)} %get-tuple-element.19, f32[16,24,1023]{2,1,0:T(8,128)S(1)} %get-tuple-element.127, f32[16,24,1]{2,1,0:T(8,128)S(1)} %get-tuple-element.129, f32[16,24,1]{2,1,0:T(8,128)S(1)} %get-tuple-element.130, f32[16,24,1023]{2,1,0:T(8,128)S(1)} %get-tuple-element.128, ...), kind=kLoop, calls=%fused_computation.7 | loop fusion | flops 5898240 | bytes 11206657 | tf_op jit(solution)/shard_map/jit(_where)/select_n | solution.py:113
  36.0 0.7 fusion.168
  36.7 1.2 %add_select_fusion.7 = f32[16,24,1024]{2,1,0:T(8,128)S(1)} fusion(f32[16,26,1024]{2,1,0:T(8,128)S(1)} %get-tuple-element.18, f32[16,24,1023]{2,1,0:T(8,128)S(1)} %get-tuple-element.25, f32[16,24,1]{2,1,0:T(8,128)S(1)} %get-tuple-element.27, f32[16,24,1]{2,1,0:T(8,128)S(1)} %get-tuple-element.26, f32[16,24,1023]{2,1,0:T(8,128)S(1)} %get-tuple-element.24, ...), kind=kLoop, calls=%fused_computation.8 | loop fusion | flops 5505024 | bytes 11206657 | tf_op jit(solution)/shard_map/jit(_where)/select_n | solution.py:112
  38.0 1.3 %add_select_fusion.4 = f32[16,22,1024]{2,1,0:T(8,128)S(1)} fusion(f32[16,24,1024]{2,1,0:T(8,128)S(1)} %add_select_fusion.6, f32[16,22,1023]{2,1,0:T(8,128)S(1)} %get-tuple-element.61, f32[16,22,1]{2,1,0:T(8,128)S(1)} %get-tuple-element.63, f32[16,22,1]{2,1,0:T(8,128)S(1)} %get-tuple-element.62, f32[16,22,1023]{2,1,0:T(8,128)S(1)} %get-tuple-element.60, ...), kind=kLoop, calls=%fused_computation.5 | loop fusion | flops 5406720 | bytes 10272769 | tf_op jit(solution)/shard_map/jit(_where)/select_n | solution.py:113
  39.4 0.7 fusion.166
  40.1 0.7 fusion.164
  40.8 1.5 %add_select_fusion.5 = f32[16,22,1024]{2,1,0:T(8,128)S(1)} fusion(f32[16,24,1024]{2,1,0:T(8,128)S(1)} %add_select_fusion.7, f32[16,22,1023]{2,1,0:T(8,128)S(1)} %get-tuple-element.53, f32[16,22,1]{2,1,0:T(8,128)S(1)} %get-tuple-element.55, f32[16,22,1]{2,1,0:T(8,128)S(1)} %get-tuple-element.54, f32[16,22,1023]{2,1,0:T(8,128)S(1)} %get-tuple-element.52, ...), kind=kLoop, calls=%fused_computation.6 | loop fusion | flops 5046272 | bytes 10272769 | tf_op jit(solution)/shard_map/jit(_where)/select_n | solution.py:112
  42.5 1.3 %add_select_fusion.2 = f32[16,20,1024]{2,1,0:T(8,128)S(1)} fusion(f32[16,22,1024]{2,1,0:T(8,128)S(1)} %add_select_fusion.4, f32[16,20,1023]{2,1,0:T(8,128)S(1)} %get-tuple-element.57, f32[16,20,1]{2,1,0:T(8,128)S(1)} %get-tuple-element.59, f32[16,20,1]{2,1,0:T(8,128)S(1)} %get-tuple-element.58, f32[16,20,1023]{2,1,0:T(8,128)S(1)} %get-tuple-element.56, ...), kind=kLoop, calls=%fused_computation.3 | loop fusion | flops 4915200 | bytes 9338881 | tf_op jit(solution)/shard_map/jit(_where)/select_n | solution.py:113
  43.9 0.7 fusion.162
  44.6 0.7 fusion.160
  45.3 1.3 %add_select_fusion.3 = f32[16,20,1024]{2,1,0:T(8,128)S(1)} fusion(f32[16,22,1024]{2,1,0:T(8,128)S(1)} %add_select_fusion.5, f32[16,20,1023]{2,1,0:T(8,128)S(1)} %get-tuple-element.45, f32[16,20,1]{2,1,0:T(8,128)S(1)} %get-tuple-element.47, f32[16,20,1]{2,1,0:T(8,128)S(1)} %get-tuple-element.46, f32[16,20,1023]{2,1,0:T(8,128)S(1)} %get-tuple-element.44, ...), kind=kLoop, calls=%fused_computation.4 | loop fusion | flops 4587520 | bytes 9338881 | tf_op jit(solution)/shard_map/jit(_where)/select_n | solution.py:112
  46.7 0.7 fusion.156
  47.4 1.3 %add_select_fusion = f32[16,18,1024]{2,1,0:T(8,128)S(1)} fusion(f32[16,20,1024]{2,1,0:T(8,128)S(1)} %add_select_fusion.2, f32[16,18,1023]{2,1,0:T(8,128)S(1)} %get-tuple-element.49, f32[16,18,1]{2,1,0:T(8,128)S(1)} %get-tuple-element.51, f32[16,18,1]{2,1,0:T(8,128)S(1)} %get-tuple-element.50, f32[16,18,1023]{2,1,0:T(8,128)S(1)} %get-tuple-element.48, ...), kind=kLoop, calls=%fused_computation.1 | loop fusion | flops 4423680 | bytes 8404993 | tf_op jit(solution)/shard_map/jit(_where)/select_n | solution.py:113
  48.9 1.3 %add_select_fusion.1 = f32[16,18,1024]{2,1,0:T(8,128)S(1)} fusion(f32[16,20,1024]{2,1,0:T(8,128)S(1)} %add_select_fusion.3, f32[16,18,1023]{2,1,0:T(8,128)S(1)} %get-tuple-element.37, f32[16,18,1]{2,1,0:T(8,128)S(1)} %get-tuple-element.39, f32[16,18,1]{2,1,0:T(8,128)S(1)} %get-tuple-element.38, f32[16,18,1023]{2,1,0:T(8,128)S(1)} %get-tuple-element.36, ...), kind=kLoop, calls=%fused_computation.2 | loop fusion | flops 4128768 | bytes 8404993 | tf_op jit(solution)/shard_map/jit(_where)/select_n | solution.py:112
  50.5 0.5 fusion.158
  51.0 0.5 fusion.154
  51.4 0.8 fusion.59
  52.3 0.8 fusion.60
  53.1 0.2 pad_maximum_fusion.3
  53.3 0.1 copy.39
  53.7 7.7 %collective-permute-done.3 = f32[34,16,1024]{2,1,0:T(8,128)S(1)} collective-permute-done((f32[34,16,1024]{2,1,0:T(8,128)S(1)}, f32[34,16,1024]{2,1,0:T(8,128)S(1)}, u32[]{:S(2)}, u32[]{:S(2)}) %collective-permute-start.3) | collective-permute-done | bytes 2228256 | tf_op jit(solution)/shard_map/ppermute | solution.py:49
  61.4 0.6 multiply_reduce_fusion.1
  62.0 0.4 fusion.1
  62.5 3.1 %fusion.56 = f32[16,16]{1,0:T(8,128)S(1)} fusion(f32[16,2,16,1024]{3,2,1,0:T(8,128)S(1)} %bitcast.145), kind=kOutput, calls=%fused_computation.86 | convolution fusion | flops 50331648 | bytes 2098176 | tf_op jit(solution)/shard_map/dot_general | solution.py:218
  65.9 1.3 %concatenate.196 = f32[290]{0:T(512)S(1)} concatenate(f32[1]{0:T(128)} %bitcast.1, f32[1]{0:T(128)} %bitcast.19, f32[16]{0:T(128)S(1)} %multiply_reduce_fusion, f32[16]{0:T(128)S(1)} %reduce_sum.67, f32[256]{0:T(256)S(1)} %reshape.100), dimensions={0} | concatenate | bytes 2320 | tf_op jit(solution)/shard_map/concatenate | solution.py:222
  67.3 3.6 %collective-permute-done.4 = f32[290]{0:T(512)S(1)} collective-permute-done((f32[290]{0:T(512)S(1)}, f32[290]{0:T(512)S(1)}, u32[]{:S(2)}, u32[]{:S(2)}) %collective-permute-start.4) | collective-permute-done | bytes 1192 | tf_op jit(solution)/shard_map/ppermute | solution.py:65
  70.9 1.2 %collective-permute-start.5 = (f32[290]{0:T(512)S(1)}, f32[290]{0:T(512)S(1)}, u32[]{:S(2)}, u32[]{:S(2)}) collective-permute-start(f32[290]{0:T(512)S(1)} %add.491), channel_id=1, source_target_pairs={{0,64},{32,96},{64,0},{96,32},{128,192},{160,224},{192,128},{224,1... | collective-permute-start | bytes 3488 | tf_op jit(solution)/shard_map/ppermute | solution.py:65
  72.1 3.3 %collective-permute-done.5 = f32[290]{0:T(512)S(1)} collective-permute-done((f32[290]{0:T(512)S(1)}, f32[290]{0:T(512)S(1)}, u32[]{:S(2)}, u32[]{:S(2)}) %collective-permute-start.5) | collective-permute-done | bytes 1192 | tf_op jit(solution)/shard_map/ppermute | solution.py:65
  75.4 3.8 %collective-permute-start.6 = (f32[290]{0:T(512)S(1)}, f32[290]{0:T(512)S(1)}, u32[]{:S(2)}, u32[]{:S(2)}) collective-permute-start(f32[290]{0:T(512)S(1)} %add.492), channel_id=1, source_target_pairs={{0,128},{32,160},{64,192},{96,224},{128,0},{160,32},{192,64},{224,... | collective-permute-start | bytes 3488 | tf_op jit(solution)/shard_map/ppermute | solution.py:65
  79.2 3.7 %collective-permute-done.6 = f32[290]{0:T(512)S(1)} collective-permute-done((f32[290]{0:T(512)S(1)}, f32[290]{0:T(512)S(1)}, u32[]{:S(2)}, u32[]{:S(2)}) %collective-permute-start.6) | collective-permute-done | bytes 1192 | tf_op jit(solution)/shard_map/ppermute | solution.py:65
  82.9 1.6 %collective-permute-start.7 = (f32[290]{0:T(512)S(1)}, f32[290]{0:T(512)S(1)}, u32[]{:S(2)}, u32[]{:S(2)}) collective-permute-start(f32[290]{0:T(512)S(1)} %add.493), channel_id=1, source_target_pairs={{0,8},{8,0},{16,24},{24,16},{1,9},{9,1},{17,25},{25,17},{2,10},{10... | collective-permute-start | bytes 3488 | tf_op jit(solution)/shard_map/ppermute | solution.py:65
  84.4 2.0 %collective-permute-done.7 = f32[290]{0:T(512)S(1)} collective-permute-done((f32[290]{0:T(512)S(1)}, f32[290]{0:T(512)S(1)}, u32[]{:S(2)}, u32[]{:S(2)}) %collective-permute-start.7) | collective-permute-done | bytes 1192 | tf_op jit(solution)/shard_map/ppermute | solution.py:65
  86.5 3.2 %collective-permute-start.8 = (f32[290]{0:T(512)S(1)}, f32[290]{0:T(512)S(1)}, u32[]{:S(2)}, u32[]{:S(2)}) collective-permute-start(f32[290]{0:T(512)S(1)} %add.494), channel_id=1, source_target_pairs={{0,16},{8,24},{16,0},{24,8},{1,17},{9,25},{17,1},{25,9},{2,18},{10... | collective-permute-start | bytes 3488 | tf_op jit(solution)/shard_map/ppermute | solution.py:65
  89.6 1.9 %collective-permute-done.8 = f32[290]{0:T(512)S(1)} collective-permute-done((f32[290]{0:T(512)S(1)}, f32[290]{0:T(512)S(1)}, u32[]{:S(2)}, u32[]{:S(2)}) %collective-permute-start.8) | collective-permute-done | bytes 1192 | tf_op jit(solution)/shard_map/ppermute | solution.py:65
  91.6 3.8 %collective-permute-start.9 = (f32[290]{0:T(512)S(1)}, f32[290]{0:T(512)S(1)}, u32[]{:S(2)}, u32[]{:S(2)}) collective-permute-start(f32[290]{0:T(512)S(1)} %add.495), channel_id=1, source_target_pairs={{0,2},{2,0},{4,6},{6,4},{1,3},{3,1},{5,7},{7,5},{8,10},{10,8},{12,... | collective-permute-start | bytes 3488 | tf_op jit(solution)/shard_map/ppermute | solution.py:65
  95.4 1.6 %collective-permute-done.9 = f32[290]{0:T(512)S(1)} collective-permute-done((f32[290]{0:T(512)S(1)}, f32[290]{0:T(512)S(1)}, u32[]{:S(2)}, u32[]{:S(2)}) %collective-permute-start.9) | collective-permute-done | bytes 1192 | tf_op jit(solution)/shard_map/ppermute | solution.py:65
  96.9 2.6 %collective-permute-start.10 = (f32[290]{0:T(512)S(1)}, f32[290]{0:T(512)S(1)}, u32[]{:S(2)}, u32[]{:S(2)}) collective-permute-start(f32[290]{0:T(512)S(1)} %add.496), channel_id=1, source_target_pairs={{0,4},{2,6},{4,0},{6,2},{1,5},{3,7},{5,1},{7,3},{8,12},{10,14},{12... | collective-permute-start | bytes 3488 | tf_op jit(solution)/shard_map/ppermute | solution.py:65
  99.5 0.3 collective-permute-start.11
  99.8 2.2 %collective-permute-done.10 = f32[290]{0:T(512)S(1)} collective-permute-done((f32[290]{0:T(512)S(1)}, f32[290]{0:T(512)S(1)}, u32[]{:S(2)}, u32[]{:S(2)}) %collective-permute-start.10) | collective-permute-done | bytes 1192 | tf_op jit(solution)/shard_map/ppermute | solution.py:65
  102.0 0.5 slice_bitcast_fusion.6.scalar_ref
  102.7 0.6 slice_bitcast_fusion.7
  103.2 0.7 reshape.101.jacobian_ref
  103.9 3.4 %shard_map.76 = (f32[1,16]{1,0:T(1,128)}, f32[1,1]{1,0:T(1,128)}) custom-call(f32[16,16]{1,0:T(8,128)} %reshape.101.jacobian_ref, f32[1,16]{1,0:T(1,128)} %get-tuple-element.122.along_ref, f32[1,16]{1,0:T(1,128)} %get-tuple-element.121.cross_ref, f32[1,2]{1,0:T(1,128)} %slice_bitcast_fusion.6.scalar_ref), custom_call_target="tpu_custom_call" | custom-call | tf_op jit(solution)/shard_map/pallas_call | solution.py:175
  107.3 1.6 %fusion = f32[2,16,1024]{2,1,0:T(8,128)} fusion(f32[1,1,16,2,16,1024]{5,4,3,2,1,0:T(8,128)S(1)} %copy-done, f32[16]{0:T(128)} %bitcast.153), kind=kLoop, calls=%fused_computation.14 | loop fusion | flops 1015808 | bytes 2228288 | tf_op jit(solution)/shard_map/reduce_sum | solution.py:240
  108.9 1.3 %multiply_bitcast_fusion = f32[1,1,2,16,1024]{4,3,2,1,0:T(8,128)} fusion(f32[2,16,1024]{2,1,0:T(8,128)S(1)} %collective-permute-done.11, f32[]{:T(128)} %bitcast.33, f32[1,1,2,16,1024]{4,3,2,1,0:T(8,128)S(1)} %copy-done.1), kind=kLoop, calls=%fused_computation.117 | loop fusion | flops 65536 | bytes 393220 | tf_op jit(solution)/shard_map/mul | solution.py:239
  (55 shorter events, 4.1 us)
Async XLA Ops:
  3.7 3.3 %copy-start.1 = (f32[1,1,2,16,1024]{4,3,2,1,0:T(8,128)S(1)}, f32[1,1,2,16,1024]{4,3,2,1,0:T(8,128)}, u32[]{:S(2)}) copy-start(f32[1,1,2,16,1024]{4,3,2,1,0:T(8,128)} %param.5) | copy-start | bytes 393220
  3.7 3.4 %copy-start = (f32[1,1,16,2,16,1024]{5,4,3,2,1,0:T(8,128)S(1)}, f32[1,1,16,2,16,1024]{5,4,3,2,1,0:T(8,128)}, u32[]{:S(2)}) copy-start(f32[1,1,16,2,16,1024]{5,4,3,2,1,0:T(8,128)} %param.6) | copy-start | bytes 6291460
  4.2 20.1 %collective-permute-start.2 = (f32[35,5,1024]{2,0,1:T(8,128)S(1)}, f32[35,5,1024]{2,0,1:T(8,128)S(1)}, u32[]{:S(2)}, u32[]{:S(2)}) collective-permute-start(f32[35,5,1024]{2,0,1:T(8,128)S(1)} %copy.36), channel_id=1, source_target_pairs={{2,0},{4,2},{6,4},{8,6},{10,8},{12,10},{14,12},{16,14},{18,16},{20... | collective-permute-start | bytes 2150408 | tf_op jit(solution)/shard_map/ppermute | solution.py:33
  6.9 21.5 %collective-permute-start.1 = (f32[35,5,1024]{2,0,1:T(8,128)S(1)}, f32[35,5,1024]{2,0,1:T(8,128)S(1)}, u32[]{:S(2)}, u32[]{:S(2)}) collective-permute-start(f32[35,5,1024]{2,0,1:T(8,128)S(1)} %copy.35), channel_id=1, source_target_pairs={{0,2},{2,4},{4,6},{6,8},{8,10},{10,12},{12,14},{14,16},{16,18},{18... | collective-permute-start | bytes 2150408 | tf_op jit(solution)/shard_map/ppermute | solution.py:31
  7.0 6.7 %collective-permute-start = (f32[2,16,1024]{2,1,0:T(8,128)S(1)}, f32[2,16,1024]{2,1,0:T(8,128)S(1)}, u32[]{:S(2)}, u32[]{:S(2)}) collective-permute-start(f32[2,16,1024]{2,1,0:T(8,128)S(1)} %bitcast.147), channel_id=1, source_target_pairs={{0,1},{1,0},{2,3},{3,2},{4,5},{5,4},{6,7},{7,6},{8,9},{9,8},{10,11... | collective-permute-start | bytes 393224 | tf_op jit(solution)/shard_map/ppermute | solution.py:43
  7.3 54.1 %collective-permute-start.3 = (f32[34,16,1024]{2,1,0:T(8,128)S(1)}, f32[34,16,1024]{2,1,0:T(8,128)S(1)}, u32[]{:S(2)}, u32[]{:S(2)}) collective-permute-start(f32[34,16,1024]{2,1,0:T(8,128)S(1)} %pad_maximum_fusion.2), channel_id=1, source_target_pairs={{32,0},{64,32},{96,64},{128,96},{160,128},{192,160},{224,192},{0,2... | collective-permute-start | bytes 6684680 | tf_op jit(solution)/shard_map/ppermute | solution.py:49
  67.3 3.6 %collective-permute-start.4 = (f32[290]{0:T(512)S(1)}, f32[290]{0:T(512)S(1)}, u32[]{:S(2)}, u32[]{:S(2)}) collective-permute-start(f32[290]{0:T(512)S(1)} %concatenate.196), channel_id=1, source_target_pairs={{0,32},{32,0},{64,96},{96,64},{128,160},{160,128},{192,224},{224,1... | collective-permute-start | bytes 3488 | tf_op jit(solution)/shard_map/ppermute | solution.py:65
  70.9 4.5 %collective-permute-start.5 = (f32[290]{0:T(512)S(1)}, f32[290]{0:T(512)S(1)}, u32[]{:S(2)}, u32[]{:S(2)}) collective-permute-start(f32[290]{0:T(512)S(1)} %add.491), channel_id=1, source_target_pairs={{0,64},{32,96},{64,0},{96,32},{128,192},{160,224},{192,128},{224,1... | collective-permute-start | bytes 3488 | tf_op jit(solution)/shard_map/ppermute | solution.py:65
  75.4 7.5 %collective-permute-start.6 = (f32[290]{0:T(512)S(1)}, f32[290]{0:T(512)S(1)}, u32[]{:S(2)}, u32[]{:S(2)}) collective-permute-start(f32[290]{0:T(512)S(1)} %add.492), channel_id=1, source_target_pairs={{0,128},{32,160},{64,192},{96,224},{128,0},{160,32},{192,64},{224,... | collective-permute-start | bytes 3488 | tf_op jit(solution)/shard_map/ppermute | solution.py:65
  82.9 3.6 %collective-permute-start.7 = (f32[290]{0:T(512)S(1)}, f32[290]{0:T(512)S(1)}, u32[]{:S(2)}, u32[]{:S(2)}) collective-permute-start(f32[290]{0:T(512)S(1)} %add.493), channel_id=1, source_target_pairs={{0,8},{8,0},{16,24},{24,16},{1,9},{9,1},{17,25},{25,17},{2,10},{10... | collective-permute-start | bytes 3488 | tf_op jit(solution)/shard_map/ppermute | solution.py:65
  86.5 5.1 %collective-permute-start.8 = (f32[290]{0:T(512)S(1)}, f32[290]{0:T(512)S(1)}, u32[]{:S(2)}, u32[]{:S(2)}) collective-permute-start(f32[290]{0:T(512)S(1)} %add.494), channel_id=1, source_target_pairs={{0,16},{8,24},{16,0},{24,8},{1,17},{9,25},{17,1},{25,9},{2,18},{10... | collective-permute-start | bytes 3488 | tf_op jit(solution)/shard_map/ppermute | solution.py:65
  91.6 5.4 %collective-permute-start.9 = (f32[290]{0:T(512)S(1)}, f32[290]{0:T(512)S(1)}, u32[]{:S(2)}, u32[]{:S(2)}) collective-permute-start(f32[290]{0:T(512)S(1)} %add.495), channel_id=1, source_target_pairs={{0,2},{2,0},{4,6},{6,4},{1,3},{3,1},{5,7},{7,5},{8,10},{10,8},{12,... | collective-permute-start | bytes 3488 | tf_op jit(solution)/shard_map/ppermute | solution.py:65
  96.9 5.1 %collective-permute-start.10 = (f32[290]{0:T(512)S(1)}, f32[290]{0:T(512)S(1)}, u32[]{:S(2)}, u32[]{:S(2)}) collective-permute-start(f32[290]{0:T(512)S(1)} %add.496), channel_id=1, source_target_pairs={{0,4},{2,6},{4,0},{6,2},{1,5},{3,7},{5,1},{7,3},{8,12},{10,14},{12... | collective-permute-start | bytes 3488 | tf_op jit(solution)/shard_map/ppermute | solution.py:65
  99.5 9.4 %collective-permute-start.11 = (f32[2,16,1024]{2,1,0:T(8,128)S(1)}, f32[2,16,1024]{2,1,0:T(8,128)S(1)}, u32[]{:S(2)}, u32[]{:S(2)}) collective-permute-start(f32[2,16,1024]{2,1,0:T(8,128)S(1)} %get-tuple-element.76), channel_id=1, source_target_pairs={{224,0},{0,32},{32,64},{64,96},{96,128},{128,160},{160,192},{192,2... | collective-permute-start | bytes 393224 | tf_op jit(solution)/shard_map/ppermute | solution.py:49

commit v2 on v1

--- a/solution.py
+++ b/solution.py
@@ -200,9 +200,23 @@
     total = 2.0 * lax.axis_size("tm") * row_count * lax.axis_size(SPACE) * column_count
     gap_part = jnp.sum(gap * gap)
     along_part = jnp.sum(panel_rows * gap[None, :], 1)
-    widened = extended_2(jnp.concatenate([stacked, feed_rate[None]], 0), ((SPACE, 1),), STEPS)
-    fields = (widened[0], widened[1], widened[2:-1:2], widened[3:-1:2])
-    feed_wide = widened[-1]
+    count = lax.axis_size(SPACE)
+    pieces = (start, tangent, feed_rate[None])
+    head = jnp.concatenate([piece[:, :STEPS] for piece in pieces], 0)
+    tail = jnp.concatenate([piece[:, -STEPS:] for piece in pieces], 0)
+    before = lax.ppermute(tail, SPACE, [(i, (i + 1) % count) for i in range(count)])
+    after = lax.ppermute(head, SPACE, [((i + 1) % count, i) for i in range(count)])
+
+    def wide(index, interior):
+        return jnp.concatenate([before[index], interior, after[index]], -2)
+
+    fields = (
+        wide(0, start[0]),
+        wide(1, start[1]),
+        wide(slice(2, -1, 2), tangent[0::2]),
+        wide(slice(3, -1, 2), tangent[1::2]),
+    )
+    feed_wide = wide(-1, feed_rate)
     total_rows = feed_wide.shape[0]
     for step_index in range(STEPS):
         fields = advance(

time: 112 us -> 129 us (1.15)
  local copies, waits for them, and re-layouts: 15.9 us -> 40.4 us
  waiting for transfers between devices: 39.3 us -> 19.6 us
  starting transfers between devices: 24.7 us -> 32.5 us
  other arithmetic: 22 us -> 26.2 us
    slice x4 -> x10, local copies, waits for them, and re-layouts: 1.76 us -> 14.7 us  [the longest x6 10.9 us: wide(): return jnp.concatenate([before[index], interior, after[index]], -2)]
    unnamed x4 -> x50, local copies, waits for them, and re-layouts: 0.01 us -> 10 us
    ppermute x2, waiting for transfers between devices: 7.71 us -> 0.01 us  [passed_along(): return lax.ppermute(block, axis, route)]
    ppermute x7, waiting for transfers between devices: 18.3 us -> 11.3 us  [one_axis_at_a_time(): x = x + lax.ppermute(x, axis, pairs)]
    ppermute x7, starting transfers between devices: 16.2 us -> 23.1 us  [one_axis_at_a_time(): x = x + lax.ppermute(x, axis, pairs)]
    ppermute x2, waiting for transfers between devices: 13.3 us -> 8.29 us  [the longest x1 7.73 us: on_device(): lax.ppermute(tail, SPACE, [(i, (i + 1) % count) for i in range(count)])]
    reduce_sum x2, other arithmetic: 0.57 us -> 2.13 us  [on_device(): jacobian_mismatch = jnp.sum(next_jacobian * next_mismatch[None, :], 1)]
    concatenate x1, other arithmetic: 0.15 us -> 1.62 us  [on_device(): stacked = jnp.concatenate([start, tangent], 0)]
  transfers between devices with their start and end apart: 12 -> 12, of which waited for: 10 -> 9; matrix products, arithmetic and copies ran while one was open for 28% -> 46% of each run, Pallas kernels for 3% -> 3%
where the time goes in v2:
time: 129 us; the launch traced here: 127 us
  local copies, waits for them, and re-layouts  40.4 us (31%)
  starting transfers between devices  32.5 us (25%)
  other arithmetic  26.2 us (20%)
  waiting for transfers between devices  19.6 us (15%)
  Pallas kernels  3.36 us (3%)
  matrix products  2.88 us (2%)
  between operations  1.95 us (2%)
    ppermute x7, starting transfers between devices, one_axis_at_a_time(): x = x + lax.ppermute(x, axis, pairs)  23.1 us
    ppermute x7, waiting for transfers between devices, one_axis_at_a_time(): x = x + lax.ppermute(x, axis, pairs)  11.3 us
    slice x6, local copies, waits for them, and re-layouts, wide(): return jnp.concatenate([before[index], interior, after[index]], -2)  10.9 us
    unnamed x50, local copies, waits for them, and re-layouts  10 us
    slice x36, local copies, waits for them, and re-layouts, laplacian_rows(): jnp.roll(interior, -1, -1)  9.79 us
    ppermute x1, waiting for transfers between devices, on_device(): lax.ppermute(tail, SPACE, [(i, (i + 1) % count) for i in range(count)])  7.73 us
    ppermute x2, starting transfers between devices, passed_along(): return lax.ppermute(block, axis, route)  6.88 us
    select_n x4, other arithmetic, advance(): jnp.where(active, new_tangent_inh, tangent_inh)  5.82 us
  transfers between devices with their start and end apart: 12, of which 9 were waited for; matrix products, arithmetic and copies ran while one was open for 46% of the time, Pallas kernels for 3%

profile of v2, /device:TPU:2, one launch (start us, length us, event | category | flops | bytes accessed | tf_op | source)
XLA Modules:
  0.0 126.9 jit_solution(14461419952346183067)
XLA Ops:
  0.7 0.9 fusion.174
  1.6 1.7 %fusion.153 = (f32[32,5,1024]{2,1,0:T(8,128)S(1)}, f32[32,5,1024]{2,1,0:T(8,128)S(1)}) fusion(f32[32,16,1024]{2,1,0:T(8,128)} %bitcast.66), kind=kLoop, calls=%fused_computation.273 | loop fusion | bytes 2621440 | tf_op jit(solution)/shard_map/slice | solution.py:206
  4.1 1.6 %collective-permute-start.1 = (f32[35,5,1024]{2,0,1:T(8,128)S(1)}, f32[35,5,1024]{2,0,1:T(8,128)S(1)}, u32[]{:S(2)}, u32[]{:S(2)}) collective-permute-start(f32[35,5,1024]{2,0,1:T(8,128)S(1)} %copy.31), channel_id=1, source_target_pairs={{0,2},{2,4},{4,6},{6,8},{8,10},{10,12},{12,14},{14,16},{16,18},{18... | collective-permute-start | bytes 2150408 | tf_op jit(solution)/shard_map/ppermute | solution.py:207
  6.2 0.9 collective-permute-start.2
  7.2 1.6 %pad_maximum_fusion = f32[34,16,1024]{2,1,0:T(8,128)} fusion(f32[32,16,1024]{2,1,0:T(8,128)S(1)} %bitcast.67, f32[2,16,1024]{2,1,0:T(8,128)S(1)} %bitcast.72), kind=kLoop, calls=%fused_computation.8 | loop fusion | flops 557056 | bytes 4456448 | tf_op jit(solution)/shard_map/concatenate | solution.py:190
  8.9 5.9 %collective-permute-start.3 = (f32[34,16,1024]{2,1,0:T(8,128)}, f32[34,16,1024]{2,1,0:T(8,128)}, u32[]{:S(2)}, u32[]{:S(2)}) collective-permute-start(f32[34,16,1024]{2,1,0:T(8,128)} %pad_maximum_fusion), channel_id=1, source_target_pairs={{32,0},{64,32},{96,64},{128,96},{160,128},{192,160},{224,192},{0,2... | collective-permute-start | bytes 6684680 | tf_op jit(solution)/shard_map/ppermute | solution.py:49
  14.7 1.2 fusion.151
  16.6 0.7 multiply_reduce_fusion.2
  17.6 7.7 %collective-permute-done.1 = f32[35,5,1024]{2,0,1:T(8,128)S(1)} collective-permute-done((f32[35,5,1024]{2,0,1:T(8,128)S(1)}, f32[35,5,1024]{2,0,1:T(8,128)S(1)}, u32[]{:S(2)}, u32[]{:S(2)}) %collective-permute-start.1) | collective-permute-done | bytes 716832 | tf_op jit(solution)/shard_map/ppermute | solution.py:207
  25.4 0.7 copy_bitcast_fusion.1
  26.7 0.7 copy_bitcast_fusion
  27.6 0.7 fusion.173
  29.5 2.7 %slice.741 = f32[16,5,1024]{2,0,1:T(8,128)} slice(f32[35,5,1024]{2,0,1:T(8,128)} %copy-done.6), slice={[2:34:2], [0:5:1], [0:1024:1]} | slice | bytes 655360 | tf_op jit(solution)/shard_map/slice | solution.py:211
  32.2 2.0 %copy.53 = f32[16,5,1024]{2,1,0:T(8,128)} copy(f32[16,5,1024]{2,0,1:T(8,128)} %slice.741) | data formatting | bytes 655360
  34.3 2.7 %slice.743 = f32[16,5,1024]{2,0,1:T(8,128)} slice(f32[35,5,1024]{2,0,1:T(8,128)} %copy-done.7), slice={[2:34:2], [0:5:1], [0:1024:1]} | slice | bytes 655360 | tf_op jit(solution)/shard_map/slice | solution.py:211
  37.0 2.0 %copy.54 = f32[16,5,1024]{2,1,0:T(8,128)} copy(f32[16,5,1024]{2,0,1:T(8,128)} %slice.743) | data formatting | bytes 655360
  39.0 2.7 %slice.751 = f32[16,5,1024]{2,0,1:T(8,128)} slice(f32[35,5,1024]{2,0,1:T(8,128)} %copy-done.6), slice={[3:34:2], [0:5:1], [0:1024:1]} | slice | bytes 655360 | tf_op jit(solution)/shard_map/slice | solution.py:211
  41.7 2.0 %copy.55 = f32[16,5,1024]{2,1,0:T(8,128)} copy(f32[16,5,1024]{2,0,1:T(8,128)} %slice.751) | data formatting | bytes 655360
  43.6 2.7 %slice.753 = f32[16,5,1024]{2,0,1:T(8,128)} slice(f32[35,5,1024]{2,0,1:T(8,128)} %copy-done.7), slice={[3:34:2], [0:5:1], [0:1024:1]} | slice | bytes 655360 | tf_op jit(solution)/shard_map/slice | solution.py:211
  46.3 1.2 copy.56
  47.5 2.5 %pad_maximum_fusion.1 = (f32[16,26,1024]{2,1,0:T(8,128)S(1)}, f32[16,26,1024]{2,1,0:T(8,128)S(1)}) fusion(f32[16,5,1024]{2,1,0:T(8,128)} %copy.54, f32[16,16,1024]{2,1,0:T(8,128)} %get-tuple-element.15, f32[16,5,1024]{2,1,0:T(8,128)} %copy.53, f32[16,5,1024]{2,1,0:T(8,128)S(1)} %copy.56, f32[16,16,1024]{2,1,0:T(8,128)S(1)} %get-tuple-element.16, ...), kind=kLoop, calls=%fused_computation.10 | loop fusion | flops 1703936 | bytes 6815744 | tf_op jit(solution)/shard_map/concatenate | solution.py:211
  50.1 0.7 fusion.150
  51.4 0.7 copy-done.1
  52.1 1.6 %add_select_fusion.7 = f32[16,24,1024]{2,1,0:T(8,128)S(1)} fusion(f32[16,5,1024]{2,1,0:T(8,128)S(1)} %copy-done.4, f32[16,16,1024]{2,1,0:T(8,128)S(1)} %copy-done.1, f32[16,5,1024]{2,1,0:T(8,128)S(1)} %copy-done.3, f32[16,26,1024]{2,1,0:T(8,128)S(1)} %get-tuple-element.128, f32[16,24,1023]{2,1,0:T(8,128)S(1)} %get-tuple-element.14, ...), kind=kLoop, calls=%fused_computation.7 | loop fusion | flops 7077888 | bytes 12907521 | tf_op jit(solution)/shard_map/jit(_where)/select_n | solution.py:112
  53.7 0.7 fusion.164
  54.6 0.7 fusion.152
  55.7 1.8 %add_select_fusion.6 = f32[16,24,1024]{2,1,0:T(8,128)S(1)} fusion(f32[16,5,1024]{2,1,0:T(8,128)S(1)} %copy.56, f32[16,16,1024]{2,1,0:T(8,128)S(1)} %get-tuple-element.16, f32[16,5,1024]{2,1,0:T(8,128)S(1)} %copy-done.2, f32[16,26,1024]{2,1,0:T(8,128)S(1)} %get-tuple-element.129, f32[16,24,1023]{2,1,0:T(8,128)S(1)} %get-tuple-element.18, ...), kind=kLoop, calls=%fused_computation.6 | loop fusion | flops 7471104 | bytes 12907521 | tf_op jit(solution)/shard_map/jit(_where)/select_n | solution.py:113
  57.7 1.3 add_select_fusion.5
  59.0 0.7 fusion.160
  59.9 0.7 fusion.168
  61.2 1.3 %add_select_fusion.4 = f32[16,22,1024]{2,1,0:T(8,128)S(1)} fusion(f32[16,24,1024]{2,1,0:T(8,128)S(1)} %add_select_fusion.6, f32[16,22,1023]{2,1,0:T(8,128)S(1)} %get-tuple-element.50, f32[16,22,1]{2,1,0:T(8,128)S(1)} %get-tuple-element.52, f32[16,22,1]{2,1,0:T(8,128)S(1)} %get-tuple-element.51, f32[16,22,1023]{2,1,0:T(8,128)S(1)} %get-tuple-element.49, ...), kind=kLoop, calls=%fused_computation.4 | loop fusion | flops 5406720 | bytes 10272769 | tf_op jit(solution)/shard_map/jit(_where)/select_n | solution.py:113
  62.6 1.3 add_select_fusion.3
  63.9 0.7 fusion.156
  64.8 0.7 fusion.166
  66.0 1.3 %add_select_fusion.2 = f32[16,20,1024]{2,1,0:T(8,128)S(1)} fusion(f32[16,22,1024]{2,1,0:T(8,128)S(1)} %add_select_fusion.4, f32[16,20,1023]{2,1,0:T(8,128)S(1)} %get-tuple-element.46, f32[16,20,1]{2,1,0:T(8,128)S(1)} %get-tuple-element.48, f32[16,20,1]{2,1,0:T(8,128)S(1)} %get-tuple-element.47, f32[16,20,1023]{2,1,0:T(8,128)S(1)} %get-tuple-element.45, ...), kind=kLoop, calls=%fused_computation.2 | loop fusion | flops 4915200 | bytes 9338881 | tf_op jit(solution)/shard_map/jit(_where)/select_n | solution.py:113
  67.3 0.7 fusion.162
  68.8 1.3 %add_select_fusion.1 = f32[16,18,1024]{2,1,0:T(8,128)S(1)} fusion(f32[16,20,1024]{2,1,0:T(8,128)S(1)} %add_select_fusion.3, f32[16,18,1023]{2,1,0:T(8,128)S(1)} %get-tuple-element.26, f32[16,18,1]{2,1,0:T(8,128)S(1)} %get-tuple-element.28, f32[16,18,1]{2,1,0:T(8,128)S(1)} %get-tuple-element.27, f32[16,18,1023]{2,1,0:T(8,128)S(1)} %get-tuple-element.25, ...), kind=kLoop, calls=%fused_computation.1 | loop fusion | flops 4128768 | bytes 8404993 | tf_op jit(solution)/shard_map/jit(_where)/select_n | solution.py:112
  70.1 1.5 %add_select_fusion = f32[16,18,1024]{2,1,0:T(8,128)S(1)} fusion(f32[16,20,1024]{2,1,0:T(8,128)S(1)} %add_select_fusion.2, f32[16,18,1023]{2,1,0:T(8,128)S(1)} %get-tuple-element.38, f32[16,18,1]{2,1,0:T(8,128)S(1)} %get-tuple-element.40, f32[16,18,1]{2,1,0:T(8,128)S(1)} %get-tuple-element.39, f32[16,18,1023]{2,1,0:T(8,128)S(1)} %get-tuple-element.37, ...), kind=kLoop, calls=%fused_computation | loop fusion | flops 4423680 | bytes 8404993 | tf_op jit(solution)/shard_map/jit(_where)/select_n | solution.py:113
  72.9 0.8 fusion.63
  73.8 0.8 fusion.64
  75.2 1.5 %multiply_reduce_fusion.1 = (f32[]{:T(128)}, f32[2,16,1024]{2,1,0:T(8,128)S(1)}, f32[2,16,1024]{2,1,0:T(8,128)S(1)}) fusion(f32[34,16,1024]{2,1,0:T(8,128)} %collective-permute-done.3, f32[1,16,1024]{2,1,0:T(8,128)S(1)} %get-tuple-element.64, f32[1,16,1024]{2,1,0:T(8,128)S(1)} %fusion.134), kind=kLoop, calls=%fused_computation.135 | loop fusion | flops 131071 | bytes 524292 | tf_op jit(solution)/shard_map/reduce_sum | solution.py:234
  76.7 2.0 %fusion.1 = (f32[32]{0:T(128)S(1)}, f32[32,16,1024]{2,1,0:T(8,128)S(1)}) fusion(f32[2,16,1024]{2,1,0:T(8,128)S(1)} %get-tuple-element.10, f32[34,16,1024]{2,1,0:T(8,128)} %collective-permute-done.3, f32[16,2,16,1024]{3,2,1,0:T(8,128)S(1)} %copy.43), kind=kLoop, calls=%fused_computation.16 | loop fusion | flops 1572832 | bytes 6422656 | tf_op jit(solution)/shard_map/reduce_sum | solution.py:233
  78.7 2.9 %fusion.60 = f32[16,16]{1,0:T(8,128)S(1)} fusion(f32[16,2,16,1024]{3,2,1,0:T(8,128)S(1)} %bitcast.69), kind=kOutput, calls=%fused_computation.100 | convolution fusion | flops 50331648 | bytes 2098176 | tf_op jit(solution)/shard_map/dot_general | solution.py:232
  81.9 1.4 %concatenate.215 = f32[290]{0:T(512)S(1)} concatenate(f32[1]{0:T(128)} %bitcast.1, f32[1]{0:T(128)} %bitcast.19, f32[16]{0:T(128)S(1)} %multiply_reduce_fusion, f32[16]{0:T(128)S(1)} %reduce_sum.67, f32[256]{0:T(256)S(1)} %reshape.93), dimensions={0} | concatenate | bytes 2320 | tf_op jit(solution)/shard_map/concatenate | solution.py:236
  83.3 1.9 %collective-permute-start.4 = (f32[290]{0:T(512)S(1)}, f32[290]{0:T(512)S(1)}, u32[]{:S(2)}, u32[]{:S(2)}) collective-permute-start(f32[290]{0:T(512)S(1)} %concatenate.215), channel_id=1, source_target_pairs={{0,32},{32,0},{64,96},{96,64},{128,160},{160,128},{192,224},{224,1... | collective-permute-start | bytes 3488 | tf_op jit(solution)/shard_map/ppermute | solution.py:65
  85.2 1.7 %collective-permute-done.4 = f32[290]{0:T(512)S(1)} collective-permute-done((f32[290]{0:T(512)S(1)}, f32[290]{0:T(512)S(1)}, u32[]{:S(2)}, u32[]{:S(2)}) %collective-permute-start.4) | collective-permute-done | bytes 1192 | tf_op jit(solution)/shard_map/ppermute | solution.py:65
  86.9 3.3 %collective-permute-start.5 = (f32[290]{0:T(512)S(1)}, f32[290]{0:T(512)S(1)}, u32[]{:S(2)}, u32[]{:S(2)}) collective-permute-start(f32[290]{0:T(512)S(1)} %add.481), channel_id=1, source_target_pairs={{0,64},{32,96},{64,0},{96,32},{128,192},{160,224},{192,128},{224,1... | collective-permute-start | bytes 3488 | tf_op jit(solution)/shard_map/ppermute | solution.py:65
  90.2 1.6 %collective-permute-done.5 = f32[290]{0:T(512)S(1)} collective-permute-done((f32[290]{0:T(512)S(1)}, f32[290]{0:T(512)S(1)}, u32[]{:S(2)}, u32[]{:S(2)}) %collective-permute-start.5) | collective-permute-done | bytes 1192 | tf_op jit(solution)/shard_map/ppermute | solution.py:65
  91.7 6.8 %collective-permute-start.6 = (f32[290]{0:T(512)S(1)}, f32[290]{0:T(512)S(1)}, u32[]{:S(2)}, u32[]{:S(2)}) collective-permute-start(f32[290]{0:T(512)S(1)} %add.482), channel_id=1, source_target_pairs={{0,128},{32,160},{64,192},{96,224},{128,0},{160,32},{192,64},{224,... | collective-permute-start | bytes 3488 | tf_op jit(solution)/shard_map/ppermute | solution.py:65
  98.6 1.6 %collective-permute-done.6 = f32[290]{0:T(512)S(1)} collective-permute-done((f32[290]{0:T(512)S(1)}, f32[290]{0:T(512)S(1)}, u32[]{:S(2)}, u32[]{:S(2)}) %collective-permute-start.6) | collective-permute-done | bytes 1192 | tf_op jit(solution)/shard_map/ppermute | solution.py:65
  100.1 1.6 %collective-permute-start.7 = (f32[290]{0:T(512)S(1)}, f32[290]{0:T(512)S(1)}, u32[]{:S(2)}, u32[]{:S(2)}) collective-permute-start(f32[290]{0:T(512)S(1)} %add.483), channel_id=1, source_target_pairs={{0,8},{8,0},{16,24},{24,16},{1,9},{9,1},{17,25},{25,17},{2,10},{10... | collective-permute-start | bytes 3488 | tf_op jit(solution)/shard_map/ppermute | solution.py:65
  101.7 2.0 %collective-permute-done.7 = f32[290]{0:T(512)S(1)} collective-permute-done((f32[290]{0:T(512)S(1)}, f32[290]{0:T(512)S(1)}, u32[]{:S(2)}, u32[]{:S(2)}) %collective-permute-start.7) | collective-permute-done | bytes 1192 | tf_op jit(solution)/shard_map/ppermute | solution.py:65
  103.7 3.2 %collective-permute-start.8 = (f32[290]{0:T(512)S(1)}, f32[290]{0:T(512)S(1)}, u32[]{:S(2)}, u32[]{:S(2)}) collective-permute-start(f32[290]{0:T(512)S(1)} %add.484), channel_id=1, source_target_pairs={{0,16},{8,24},{16,0},{24,8},{1,17},{9,25},{17,1},{25,9},{2,18},{10... | collective-permute-start | bytes 3488 | tf_op jit(solution)/shard_map/ppermute | solution.py:65
  106.9 1.9 %collective-permute-done.8 = f32[290]{0:T(512)S(1)} collective-permute-done((f32[290]{0:T(512)S(1)}, f32[290]{0:T(512)S(1)}, u32[]{:S(2)}, u32[]{:S(2)}) %collective-permute-start.8) | collective-permute-done | bytes 1192 | tf_op jit(solution)/shard_map/ppermute | solution.py:65
  108.8 3.2 %collective-permute-start.9 = (f32[290]{0:T(512)S(1)}, f32[290]{0:T(512)S(1)}, u32[]{:S(2)}, u32[]{:S(2)}) collective-permute-start(f32[290]{0:T(512)S(1)} %add.485), channel_id=1, source_target_pairs={{0,2},{2,0},{4,6},{6,4},{1,3},{3,1},{5,7},{7,5},{8,10},{10,8},{12,... | collective-permute-start | bytes 3488 | tf_op jit(solution)/shard_map/ppermute | solution.py:65
  112.1 1.6 %collective-permute-done.9 = f32[290]{0:T(512)S(1)} collective-permute-done((f32[290]{0:T(512)S(1)}, f32[290]{0:T(512)S(1)}, u32[]{:S(2)}, u32[]{:S(2)}) %collective-permute-start.9) | collective-permute-done | bytes 1192 | tf_op jit(solution)/shard_map/ppermute | solution.py:65
  113.6 3.0 %collective-permute-start.10 = (f32[290]{0:T(512)S(1)}, f32[290]{0:T(512)S(1)}, u32[]{:S(2)}, u32[]{:S(2)}) collective-permute-start(f32[290]{0:T(512)S(1)} %add.486), channel_id=1, source_target_pairs={{0,4},{2,6},{4,0},{6,2},{1,5},{3,7},{5,1},{7,3},{8,12},{10,14},{12... | collective-permute-start | bytes 3488 | tf_op jit(solution)/shard_map/ppermute | solution.py:65
  116.6 1.0 collective-permute-start.11
  117.7 1.1 collective-permute-done.10
  118.8 0.6 slice_bitcast_fusion.3
  120.0 0.7 reshape.94.jacobian_ref
  120.7 3.4 %shard_map.76 = (f32[1,16]{1,0:T(1,128)}, f32[1,1]{1,0:T(1,128)}) custom-call(f32[16,16]{1,0:T(8,128)} %reshape.94.jacobian_ref, f32[1,16]{1,0:T(1,128)} %get-tuple-element.123.along_ref, f32[1,16]{1,0:T(1,128)} %get-tuple-element.122.cross_ref, f32[1,2]{1,0:T(1,128)} %slice_bitcast_fusion.2.scalar_ref), custom_call_target="tpu_custom_call" | custom-call | tf_op jit(solution)/shard_map/pallas_call | solution.py:175
  124.0 1.6 %fusion = f32[2,16,1024]{2,1,0:T(8,128)} fusion(f32[1,1,16,2,16,1024]{5,4,3,2,1,0:T(8,128)S(1)} %copy-done, f32[16]{0:T(128)} %bitcast.79), kind=kLoop, calls=%fused_computation.14 | loop fusion | flops 1015808 | bytes 2228288 | tf_op jit(solution)/shard_map/reduce_sum | solution.py:254
  125.6 1.3 %multiply_bitcast_fusion = f32[1,1,2,16,1024]{4,3,2,1,0:T(8,128)} fusion(f32[2,16,1024]{2,1,0:T(8,128)S(1)} %collective-permute-done.11, f32[]{:T(128)} %bitcast.30, f32[1,1,2,16,1024]{4,3,2,1,0:T(8,128)S(1)} %copy-done.5), kind=kLoop, calls=%fused_computation.134 | loop fusion | flops 65536 | bytes 393220 | tf_op jit(solution)/shard_map/mul | solution.py:253
  (114 shorter events, 10.1 us)
Async XLA Ops:
  0.6 16.0 %collective-permute-start = (f32[2,16,1024]{2,1,0:T(8,128)}, f32[2,16,1024]{2,1,0:T(8,128)S(1)}, u32[]{:S(2)}, u32[]{:S(2)}) collective-permute-start(f32[2,16,1024]{2,1,0:T(8,128)} %bitcast.70), channel_id=1, source_target_pairs={{0,1},{1,0},{2,3},{3,2},{4,5},{5,4},{6,7},{7,6},{8,9},{9,8},{10,11... | collective-permute-start | bytes 393224 | tf_op jit(solution)/shard_map/ppermute | solution.py:43
  1.6 1.8 %copy-start.20 = (s32[16,1024]{1,0:T(8,128)S(1)}, s32[16,1024]{1,0:T(8,128)}, u32[]{:S(2)}) copy-start(s32[16,1024]{1,0:T(8,128)} %param.7) | copy-start | bytes 196612
  1.6 1.8 %copy-start.21 = (f32[6]{0:T(128)S(1)}, f32[6]{0:T(128)}, u32[]{:S(2)}) copy-start(f32[6]{0:T(128)} %param.8) | copy-start | bytes 76
  4.1 21.2 %collective-permute-start.1 = (f32[35,5,1024]{2,0,1:T(8,128)S(1)}, f32[35,5,1024]{2,0,1:T(8,128)S(1)}, u32[]{:S(2)}, u32[]{:S(2)}) collective-permute-start(f32[35,5,1024]{2,0,1:T(8,128)S(1)} %copy.31), channel_id=1, source_target_pairs={{0,2},{2,4},{4,6},{6,8},{8,10},{10,12},{12,14},{14,16},{16,18},{18... | collective-permute-start | bytes 2150408 | tf_op jit(solution)/shard_map/ppermute | solution.py:207
  5.7 1.6 %copy-start = (f32[1,1,16,2,16,1024]{5,4,3,2,1,0:T(8,128)S(1)}, f32[1,1,16,2,16,1024]{5,4,3,2,1,0:T(8,128)}, u32[]{:S(2)}) copy-start(f32[1,1,16,2,16,1024]{5,4,3,2,1,0:T(8,128)} %param.6) | copy-start | bytes 6291460
  5.7 1.6 %copy-start.5 = (f32[1,1,2,16,1024]{4,3,2,1,0:T(8,128)S(1)}, f32[1,1,2,16,1024]{4,3,2,1,0:T(8,128)}, u32[]{:S(2)}) copy-start(f32[1,1,2,16,1024]{4,3,2,1,0:T(8,128)} %param.5) | copy-start | bytes 393220
  6.2 20.4 %collective-permute-start.2 = (f32[35,5,1024]{2,0,1:T(8,128)S(1)}, f32[35,5,1024]{2,0,1:T(8,128)S(1)}, u32[]{:S(2)}, u32[]{:S(2)}) collective-permute-start(f32[35,5,1024]{2,0,1:T(8,128)S(1)} %copy.33), channel_id=1, source_target_pairs={{2,0},{4,2},{6,4},{8,6},{10,8},{12,10},{14,12},{16,14},{18,16},{20... | collective-permute-start | bytes 2150408 | tf_op jit(solution)/shard_map/ppermute | solution.py:208
  8.9 66.3 %collective-permute-start.3 = (f32[34,16,1024]{2,1,0:T(8,128)}, f32[34,16,1024]{2,1,0:T(8,128)}, u32[]{:S(2)}, u32[]{:S(2)}) collective-permute-start(f32[34,16,1024]{2,1,0:T(8,128)} %pad_maximum_fusion), channel_id=1, source_target_pairs={{32,0},{64,32},{96,64},{128,96},{160,128},{192,160},{224,192},{0,2... | collective-permute-start | bytes 6684680 | tf_op jit(solution)/shard_map/ppermute | solution.py:49
  16.6 11.0 %copy-start.8 = (f32[16,1024]{1,0:T(8,128)}, f32[16,1024]{1,0:T(8,128)S(1)}, u32[]{:S(2)}) copy-start(f32[16,1024]{1,0:T(8,128)S(1)} %get-tuple-element.79) | copy-start | bytes 196612
  25.3 2.1 %copy-start.6 = (f32[35,5,1024]{2,0,1:T(8,128)}, f32[35,5,1024]{2,0,1:T(8,128)S(1)}, u32[]{:S(2)}) copy-start(f32[35,5,1024]{2,0,1:T(8,128)S(1)} %collective-permute-done.1) | copy-start | bytes 2150404
  26.1 2.3 %copy-start.12 = (f32[5,1024]{1,0:T(8,128)}, f32[5,1024]{1,0:T(8,128)S(1)}, u32[]{:S(2)}) copy-start(f32[5,1024]{1,0:T(8,128)S(1)} %get-tuple-element.126) | copy-start | bytes 61444
  26.6 0.9 copy-start.7
  27.4 0.9 copy-start.14
  50.0 0.8 copy-start.16
  50.0 0.8 copy-start.17
  50.0 0.9 copy-start.9
  50.0 0.9 copy-start.10
  50.1 1.0 copy-start.11
  50.1 1.0 copy-start.13
  50.1 1.0 copy-start.15
  50.1 1.2 copy-start.3
  50.1 1.3 %copy-start.4 = (f32[16,5,1024]{2,1,0:T(8,128)S(1)}, f32[16,5,1024]{2,1,0:T(8,128)}, u32[]{:S(2)}) copy-start(f32[16,5,1024]{2,1,0:T(8,128)} %copy.54) | copy-start | bytes 983044
  50.8 1.3 %copy-start.1 = (f32[16,16,1024]{2,1,0:T(8,128)S(1)}, f32[16,16,1024]{2,1,0:T(8,128)}, u32[]{:S(2)}) copy-start(f32[16,16,1024]{2,1,0:T(8,128)} %get-tuple-element.15) | copy-start | bytes 3145732
  54.6 1.0 copy-start.18
  54.6 1.0 copy-start.19
  54.6 1.1 copy-start.2
  83.3 3.6 %collective-permute-start.4 = (f32[290]{0:T(512)S(1)}, f32[290]{0:T(512)S(1)}, u32[]{:S(2)}, u32[]{:S(2)}) collective-permute-start(f32[290]{0:T(512)S(1)} %concatenate.215), channel_id=1, source_target_pairs={{0,32},{32,0},{64,96},{96,64},{128,160},{160,128},{192,224},{224,1... | collective-permute-start | bytes 3488 | tf_op jit(solution)/shard_map/ppermute | solution.py:65
  86.9 4.8 %collective-permute-start.5 = (f32[290]{0:T(512)S(1)}, f32[290]{0:T(512)S(1)}, u32[]{:S(2)}, u32[]{:S(2)}) collective-permute-start(f32[290]{0:T(512)S(1)} %add.481), channel_id=1, source_target_pairs={{0,64},{32,96},{64,0},{96,32},{128,192},{160,224},{192,128},{224,1... | collective-permute-start | bytes 3488 | tf_op jit(solution)/shard_map/ppermute | solution.py:65
  91.7 8.4 %collective-permute-start.6 = (f32[290]{0:T(512)S(1)}, f32[290]{0:T(512)S(1)}, u32[]{:S(2)}, u32[]{:S(2)}) collective-permute-start(f32[290]{0:T(512)S(1)} %add.482), channel_id=1, source_target_pairs={{0,128},{32,160},{64,192},{96,224},{128,0},{160,32},{192,64},{224,... | collective-permute-start | bytes 3488 | tf_op jit(solution)/shard_map/ppermute | solution.py:65
  100.1 3.6 %collective-permute-start.7 = (f32[290]{0:T(512)S(1)}, f32[290]{0:T(512)S(1)}, u32[]{:S(2)}, u32[]{:S(2)}) collective-permute-start(f32[290]{0:T(512)S(1)} %add.483), channel_id=1, source_target_pairs={{0,8},{8,0},{16,24},{24,16},{1,9},{9,1},{17,25},{25,17},{2,10},{10... | collective-permute-start | bytes 3488 | tf_op jit(solution)/shard_map/ppermute | solution.py:65
  103.7 5.1 %collective-permute-start.8 = (f32[290]{0:T(512)S(1)}, f32[290]{0:T(512)S(1)}, u32[]{:S(2)}, u32[]{:S(2)}) collective-permute-start(f32[290]{0:T(512)S(1)} %add.484), channel_id=1, source_target_pairs={{0,16},{8,24},{16,0},{24,8},{1,17},{9,25},{17,1},{25,9},{2,18},{10... | collective-permute-start | bytes 3488 | tf_op jit(solution)/shard_map/ppermute | solution.py:65
  108.8 4.8 %collective-permute-start.9 = (f32[290]{0:T(512)S(1)}, f32[290]{0:T(512)S(1)}, u32[]{:S(2)}, u32[]{:S(2)}) collective-permute-start(f32[290]{0:T(512)S(1)} %add.485), channel_id=1, source_target_pairs={{0,2},{2,0},{4,6},{6,4},{1,3},{3,1},{5,7},{7,5},{8,10},{10,8},{12,... | collective-permute-start | bytes 3488 | tf_op jit(solution)/shard_map/ppermute | solution.py:65
  113.6 5.1 %collective-permute-start.10 = (f32[290]{0:T(512)S(1)}, f32[290]{0:T(512)S(1)}, u32[]{:S(2)}, u32[]{:S(2)}) collective-permute-start(f32[290]{0:T(512)S(1)} %add.486), channel_id=1, source_target_pairs={{0,4},{2,6},{4,0},{6,2},{1,5},{3,7},{5,1},{7,3},{8,12},{10,14},{12... | collective-permute-start | bytes 3488 | tf_op jit(solution)/shard_map/ppermute | solution.py:65
  116.6 9.0 %collective-permute-start.11 = (f32[2,16,1024]{2,1,0:T(8,128)S(1)}, f32[2,16,1024]{2,1,0:T(8,128)S(1)}, u32[]{:S(2)}, u32[]{:S(2)}) collective-permute-start(f32[2,16,1024]{2,1,0:T(8,128)S(1)} %get-tuple-element.75), channel_id=1, source_target_pairs={{224,0},{0,32},{32,64},{64,96},{96,128},{128,160},{160,192},{192,2... | collective-permute-start | bytes 393224 | tf_op jit(solution)/shard_map/ppermute | solution.py:49
